TPU v7x, 512 devices: a whole 4x8x8 slice. The times are simulated.
512 devices in a mesh: section: 8 (over x, core), ctx: 64 (over z, y).
Axes of the slice: x: 4, y: 8, z: 8, core: 2. Of those that a mesh axis runs over, the one named last changes fastest.
Arguments:
- inputs: bfloat16 [8, 1024, 8192], P('section', None, 'ctx'), may hold values from -6 to 6
- out_grad: bfloat16 [1024, 8192], P(None, 'ctx'), may hold values from -6 to 6
- filters: bfloat16 [8, 1024, 8192], P('section', 'ctx'), may hold values from -0.0625 to 0.0625
- conv_taps: float32 [8, 3, 7, 1024], P('section'), may hold values from -2.5 to 2.5
Outputs:
- in_grad: bfloat16 [8, 1024, 8192], P('section', None, 'ctx')
- filter_grad: float32 [8, 1024, 8192], P('section', 'ctx')
- tap_grad: float32 [8, 3, 7, 1024], P('section', None, None, 'ctx')
All inputs are finite; a program needn't handle non-finite values.
Results may differ from a plain program's by a relative error of at most 0.014.
Values may be sent and summed in bfloat16 or wider, within the bound.
No kernel may reach another device: no remote copies, remote signals or barrier semaphores. Data moves between devices by JAX's collectives and lax.ppermute only.
A program may use at most 64 MiB of HBM per device.

v0:
```python
import math

import jax
import jax.numpy as jnp
from jax import lax
from jax.experimental import pallas as pl
from jax.experimental.pallas import tpu as pltpu
from jax.sharding import PartitionSpec as P

LANES = 128


def angle_table(row_count, col_count, modulus):
    row_ids = lax.broadcasted_iota(jnp.int32, (row_count, col_count), 0)
    col_ids = lax.broadcasted_iota(jnp.int32, (row_count, col_count), 1)
    product_mod = row_ids * col_ids % modulus
    angles = product_mod.astype(jnp.float32) * (2.0 * math.pi / modulus)
    return (jnp.cos(angles), jnp.sin(angles))


def split_bf16(value):
    high = value.astype(jnp.bfloat16)
    low = (value - high.astype(jnp.float32)).astype(jnp.bfloat16)
    return high, low


def split_table(value):
    high = lax.reduce_precision(value, exponent_bits=8, mantissa_bits=7)
    return high.astype(jnp.bfloat16), (value - high).astype(jnp.bfloat16)


def mat(a, b):
    return jnp.dot(a, b, preferred_element_type=jnp.float32)


def dot_left(t_hi, t_lo, value):
    v_hi, v_lo = split_bf16(value)
    return mat(t_hi, v_hi) + mat(t_hi, v_lo) + mat(t_lo, v_hi)


def dot_right(value, t_hi, t_lo):
    v_hi, v_lo = split_bf16(value)
    return mat(v_hi, t_hi) + mat(v_lo, t_hi) + mat(v_hi, t_lo)


def spectrum_tables(length):
    half = length // LANES
    blocks = 2 * half
    total = blocks * LANES
    cos_one, sin_one = angle_table(blocks, half, blocks)
    cos_tw, sin_tw = angle_table(blocks, LANES, total)
    cos_two, sin_two = angle_table(LANES, LANES, LANES)
    first = jnp.concatenate([cos_one, -sin_one], axis=0)
    forward = jnp.concatenate(
        [jnp.concatenate([cos_two, -sin_two], 1), jnp.concatenate([sin_two, cos_two], 1)], 0
    )
    backward = jnp.concatenate(
        [jnp.concatenate([cos_two, sin_two], 1), jnp.concatenate([-sin_two, cos_two], 1)], 0
    )
    last = jnp.concatenate([cos_one.T, -sin_one.T], axis=1) / total
    return (
        *split_table(first),
        cos_tw,
        sin_tw,
        *split_table(forward),
        *split_table(backward),
        *split_table(last),
    )


def chain_kernel(
    sub, taps_ref, x_ref, h_ref, og_ref, a1h, a1l, tcr, tsr, w2h, w2l, wbh, wbl, a3h, a3l,
    in_ref, fg_ref, tp_ref, q_s, k_s, v_s, conv_s, hs_s, ws_s, ds_s,
):
    layers, rows, lanes = x_ref.shape
    half = rows // sub
    blocks = 2 * half
    row_id = lax.broadcasted_iota(jnp.int32, (rows, lanes), 0)
    lane_id = lax.broadcasted_iota(jnp.int32, (rows, lanes), 1)
    first_row = row_id == 0
    last_row = row_id == half - 1
    for c in range(1, sub):
        first_row = first_row | (row_id == c * half)
        last_row = last_row | (row_id == c * half + half - 1)

    def fft(signal):
        twc = tcr[...]
        tws = tsr[...]
        parts = []
        for c in range(sub):
            y = dot_left(a1h[...], a1l[...], signal[c * half:(c + 1) * half, :])
            yr, yi = y[:blocks], y[blocks:]
            parts.append(jnp.concatenate([yr * twc + yi * tws, yi * twc - yr * tws], axis=1))
        return dot_right(jnp.concatenate(parts, axis=0), w2h[...], w2l[...])

    def ifft(spec):
        twc = tcr[...]
        tws = tsr[...]
        p = dot_right(spec, wbh[...], wbl[...])
        outs = []
        for c in range(sub):
            pr = p[c * blocks:(c + 1) * blocks, :lanes]
            pi = p[c * blocks:(c + 1) * blocks, lanes:]
            q = jnp.concatenate([pr * twc - pi * tws, pr * tws + pi * twc], axis=0)
            outs.append(dot_left(a3h[...], a3l[...], q))
        return jnp.concatenate(outs, axis=0)

    def back(value, j):
        if j == 0:
            return value
        r1 = pltpu.roll(value, j, 1)
        r2 = pltpu.roll(r1, 1, 0)
        out = jnp.where(lane_id >= j, r1, r2)
        return jnp.where(first_row & (lane_id < j), 0.0, out)

    def ahead(value, j):
        if j == 0:
            return value
        r1 = pltpu.roll(value, lanes - j, 1)
        r2 = pltpu.roll(r1, rows - 1, 0)
        out = jnp.where(lane_id < lanes - j, r1, r2)
        return jnp.where(last_row & (lane_id >= lanes - j), 0.0, out)

    def tap(layer, i, j):
        base = ((layer * 3 + i) * 7 + j) * sub
        w = jnp.full((rows, lanes), taps_ref[base + sub - 1], jnp.float32)
        for c in range(sub - 2, -1, -1):
            w = jnp.where(row_id < (c + 1) * half, taps_ref[base + c], w)
        return w

    def real_imag(spec):
        return spec[:, :lanes], spec[:, lanes:]

    def phase_one(layer, carry):
        x = x_ref[layer].astype(jnp.float32)
        feats = [jnp.zeros((rows, lanes), jnp.float32) for _ in range(3)]
        for j in range(7):
            xs = back(x, j)
            for i in range(3):
                feats[i] = feats[i] + tap(layer, i, j) * xs
        q, k, v = [f.astype(jnp.bfloat16).astype(jnp.float32) for f in feats]
        q_s[layer] = q
        k_s[layer] = k
        v_s[layer] = v
        hspec = fft(h_ref[layer].astype(jnp.float32))
        wspec = fft(k * v)
        hs_s[layer] = hspec
        ws_s[layer] = wspec
        hr, hi = real_imag(hspec)
        wr, wi = real_imag(wspec)
        conv_s[layer] = ifft(jnp.concatenate([hr * wr - hi * wi, hr * wi + hi * wr], axis=1))
        return carry

    lax.fori_loop(0, layers, phase_one, 0)

    def phase_two(step, carried):
        layer = layers - 1 - step
        grad_z = carried * q_s[layer]
        grad_q = carried * conv_s[layer]
        dspec = fft(grad_z)
        ds_s[layer] = dspec
        hr, hi = real_imag(hs_s[layer])
        dr, di = real_imag(dspec)
        grad_w = ifft(jnp.concatenate([hr * dr + hi * di, hr * di - hi * dr], axis=1))
        grads = (grad_q, grad_w * v_s[layer], grad_w * k_s[layer])
        summed = jnp.zeros((rows, lanes), jnp.float32)
        for j in range(7):
            term = tap(layer, 0, j) * ahead(grads[0], j)
            term = term + tap(layer, 1, j) * ahead(grads[1], j)
            term = term + tap(layer, 2, j) * ahead(grads[2], j)
            summed = summed + term
        rounded = summed.astype(jnp.bfloat16)
        in_ref[layer] = rounded
        x = x_ref[layer].astype(jnp.float32)
        for j in range(7):
            xs = back(x, j)
            for i in range(3):
                prod = grads[i] * xs
                for c in range(sub):
                    row = (i * 7 + j) * sub + c
                    part = jnp.sum(prod[c * half:(c + 1) * half, :], axis=0, keepdims=True)
                    tp_ref[layer, pl.ds(row, 1), :] = part
        return rounded.astype(jnp.float32)

    lax.fori_loop(0, layers, phase_two, og_ref[...].astype(jnp.float32))

    def phase_three(layer, carry):
        wr, wi = real_imag(ws_s[layer])
        dr, di = real_imag(ds_s[layer])
        fg_ref[layer] = ifft(jnp.concatenate([wr * dr + wi * di, wr * di - wi * dr], axis=1))
        return carry

    lax.fori_loop(0, layers, phase_three, 0)


def run_chain(x_all, h_all, og, taps_all):
    layers, sub, length = x_all.shape
    half = length // LANES
    rows = sub * half
    blocks = 2 * half
    tables = spectrum_tables(length)
    vmem = pl.BlockSpec(memory_space=pltpu.VMEM)
    spec_shape = pltpu.VMEM((layers, sub * blocks, 2 * LANES), jnp.float32)
    sig_shape = pltpu.VMEM((layers, rows, LANES), jnp.float32)
    in_k, fg_k, tp_k = pl.pallas_call(
        lambda *refs: chain_kernel(sub, *refs),
        out_shape=(
            jax.ShapeDtypeStruct((layers, rows, LANES), jnp.bfloat16),
            jax.ShapeDtypeStruct((layers, rows, LANES), jnp.float32),
            jax.ShapeDtypeStruct((layers, 21 * sub, LANES), jnp.float32),
        ),
        in_specs=[pl.BlockSpec(memory_space=pltpu.SMEM)] + [vmem] * 13,
        out_specs=(vmem, vmem, vmem),
        scratch_shapes=[sig_shape] * 4 + [spec_shape] * 3,
        compiler_params=pltpu.CompilerParams(vmem_limit_bytes=48 * 1024 * 1024),
        name="hyena_chain",
    )(
        taps_all.reshape(-1),
        x_all.reshape(layers, rows, LANES),
        h_all.reshape(layers, rows, LANES),
        og.reshape(rows, LANES),
        *tables,
    )
    tap_grad = jnp.sum(tp_k, axis=2).reshape(layers, 3, 7, sub)
    return in_k.reshape(layers, sub, length), fg_k.reshape(layers, sub, length), tap_grad


def shards(inputs, out_grad, filters, conv_taps):
    sec_n = lax.axis_size("section")
    ctx_n = lax.axis_size("ctx")
    sec = lax.axis_index("section")
    ctx = lax.axis_index("ctx")
    channels = filters.shape[1]
    length = filters.shape[2]
    sub = channels // sec_n
    tok_dev = inputs.shape[2]
    x_ctx = lax.all_to_all(inputs, "ctx", split_axis=1, concat_axis=2, tiled=True)[0]
    x_all = lax.all_to_all(
        x_ctx.reshape(sec_n, sub, length), "section", split_axis=0, concat_axis=0, tiled=True
    )
    h_all = lax.all_to_all(
        filters[0].reshape(sec_n, sub, length), "section", split_axis=0, concat_axis=0, tiled=True
    )
    taps_c = lax.dynamic_slice_in_dim(conv_taps[0], ctx * channels, channels, 2)
    taps_c = jnp.moveaxis(taps_c.reshape(3, 7, sec_n, sub), 2, 0)
    taps_all = lax.all_to_all(taps_c, "section", split_axis=0, concat_axis=0, tiled=True)
    og = lax.dynamic_index_in_dim(
        out_grad.reshape(ctx_n, sec_n, sub, tok_dev), sec, 1, keepdims=False
    )
    og = lax.all_to_all(og, "ctx", split_axis=0, concat_axis=2, tiled=True)[0]
    in_all, filter_grad, tap_grad = run_chain(x_all, h_all, og, taps_all)
    fg = lax.all_to_all(filter_grad, "section", split_axis=0, concat_axis=1, tiled=True)
    tg = lax.all_to_all(tap_grad, "section", split_axis=0, concat_axis=3, tiled=True)
    ig = lax.all_to_all(in_all, "section", split_axis=0, concat_axis=1, tiled=True)[0]
    ig = lax.all_to_all(ig, "ctx", split_axis=1, concat_axis=0, tiled=True)
    return (ig[None], fg, tg)


def solution(mesh):
    placed = (
        P("section", None, "ctx"),
        P(None, "ctx"),
        P("section", "ctx", None),
        P("section", None, None, None),
    )
    return jax.shard_map(
        shards,
        mesh=mesh,
        in_specs=placed,
        out_specs=(
            P("section", None, "ctx"),
            P("section", "ctx", None),
            P("section", None, None, "ctx"),
        ),
        check_vma=False,
    )
```

profile of v0, /device:TPU:8, one launch (start us, length us, event | category | flops | bytes accessed | tf_op | source)
XLA Modules:
  0.0 161.2 jit_solution(642836403346584779)
XLA Ops:
  0.7 0.8 constant_dynamic-slice_fusion
  2.2 4.3 %all-to-all-start = ((f32[8,3,7,2]{2,3,1,0:T(2,128)}), f32[8,3,7,2]{2,3,1,0:T(2,128)S(1)}, u32[]{:S(2)}, u32[]{:S(2)}) async-start(f32[8,3,7,2]{2,3,1,0:T(2,128)} %copy.53), calls=%async_computation | async-start | bytes 49152 | tf_op jit(solution)/shard_map/all_to_all | solution.py:246
  6.5 0.6 dynamic-slice_bitcast_fusion
  7.2 4.8 %all-to-all-done = f32[8,3,7,2]{2,3,1,0:T(2,128)S(1)} async-done(((f32[8,3,7,2]{2,3,1,0:T(2,128)}), f32[8,3,7,2]{2,3,1,0:T(2,128)S(1)}, u32[]{:S(2)}, u32[]{:S(2)}) %all-to-all-start) | async-done | bytes 1376 | tf_op jit(solution)/shard_map/all_to_all | solution.py:246
  11.9 16.6 %all-to-all-start.4 = ((bf16[64,2,128]{2,1,0:T(2,128)(2,1)}), bf16[64,2,128]{2,1,0:T(2,128)(2,1)S(1)}, u32[]{:S(2)}, u32[]{:S(2)}) async-start(bf16[64,2,128]{2,1,0:T(2,128)(2,1)} %dynamic-slice_bitcast_fusion), calls=%async_computation.4 | async-start | bytes 65536 | tf_op jit(solution)/shard_map/all_to_all | solution.py:250
  29.5 2.2 %reduce = bf16[1024,128]{1,0:T(8,128)(2,1)S(1)} reduce(bf16[1024,1,128]{2,1,0:T(2,128)(2,1)S(1)} %bitcast.33, bf16[]{:T(256)} %broadcast.51), dimensions={1}, to_apply=%bitcast.29.reduce_sub_computation | reduce | bytes 524290
  31.7 0.8 reshape.54
  32.4 7.0 %all-to-all-done.4 = bf16[64,2,128]{2,1,0:T(2,128)(2,1)S(1)} async-done(((bf16[64,2,128]{2,1,0:T(2,128)(2,1)}), bf16[64,2,128]{2,1,0:T(2,128)(2,1)S(1)}, u32[]{:S(2)}, u32[]{:S(2)}) %all-to-all-start.4) | async-done | bytes 32800 | tf_op jit(solution)/shard_map/all_to_all | solution.py:250
  39.5 5.8 %all-to-all-start.1 = ((bf16[64,2,1024]{2,1,0:T(2,128)(2,1)}), bf16[64,2,1024]{2,1,0:T(2,128)(2,1)S(1)}, u32[]{:S(2)}, u32[]{:S(2)}) async-start(bf16[64,2,1024]{2,1,0:T(2,128)(2,1)} %reshape.54), calls=%async_computation.1 | async-start | bytes 524288 | tf_op jit(solution)/shard_map/all_to_all | solution.py:237
  45.3 0.9 reshape_squeeze.10
  47.3 11.7 %all-to-all-done.1 = bf16[64,2,1024]{2,1,0:T(2,128)(2,1)S(1)} async-done(((bf16[64,2,1024]{2,1,0:T(2,128)(2,1)}), bf16[64,2,1024]{2,1,0:T(2,128)(2,1)S(1)}, u32[]{:S(2)}, u32[]{:S(2)}) %all-to-all-start.1) | async-done | bytes 262176 | tf_op jit(solution)/shard_map/all_to_all | solution.py:237
  59.0 3.4 %all-to-all-start.3 = ((bf16[8,2,8192]{2,1,0:T(2,128)(2,1)}), bf16[8,2,8192]{2,1,0:T(2,128)(2,1)S(1)}, u32[]{:S(2)}, u32[]{:S(2)}) async-start(bf16[8,2,8192]{2,1,0:T(2,128)(2,1)} %reshape_squeeze.10), calls=%async_computation.3 | async-start | bytes 524288 | tf_op jit(solution)/shard_map/all_to_all | solution.py:241
  63.0 0.8 reshape_squeeze.9
  63.8 6.1 %all-to-all-done.3 = bf16[8,2,8192]{2,1,0:T(2,128)(2,1)S(1)} async-done(((bf16[8,2,8192]{2,1,0:T(2,128)(2,1)}), bf16[8,2,8192]{2,1,0:T(2,128)(2,1)S(1)}, u32[]{:S(2)}, u32[]{:S(2)}) %all-to-all-start.3) | async-done | bytes 262176 | tf_op jit(solution)/shard_map/all_to_all | solution.py:241
  69.9 3.4 %all-to-all-start.2 = ((bf16[8,2,8192]{2,1,0:T(2,128)(2,1)}), bf16[8,2,8192]{2,1,0:T(2,128)(2,1)S(1)}, u32[]{:S(2)}, u32[]{:S(2)}) async-start(bf16[8,2,8192]{2,1,0:T(2,128)(2,1)} %reshape_squeeze.9), calls=%async_computation.2 | async-start | bytes 524288 | tf_op jit(solution)/shard_map/all_to_all | solution.py:238
  74.0 6.7 %all-to-all-done.2 = bf16[8,2,8192]{2,1,0:T(2,128)(2,1)S(1)} async-done(((bf16[8,2,8192]{2,1,0:T(2,128)(2,1)}), bf16[8,2,8192]{2,1,0:T(2,128)(2,1)S(1)}, u32[]{:S(2)}, u32[]{:S(2)}) %all-to-all-start.2) | async-done | bytes 262176 | tf_op jit(solution)/shard_map/all_to_all | solution.py:238
  81.0 25.6 %hyena_chain.1 = (bf16[8,128,128]{2,1,0:T(8,128)(2,1)S(1)}, f32[8,128,128]{2,1,0:T(8,128)S(1)}, f32[8,42,128]{2,1,0:T(8,128)S(1)}) custom-call(f32[336]{0:T(512)S(1)} %reshape.47.refs_0_, bf16[8,128,128]{2,1,0:T(8,128)(2,1)S(1)} %reshape.48.refs_1_, bf16[8,128,128]{2,1,0:T(8,128)(2,1)S(1)} %reshape.49.refs_2_, bf16[128,128]{1,0:T(8,128)(2,1)S(1)} %bitcast.31, ...), custom_call_target="tpu_custom_call" | custom-call | tf_op jit(solution)/shard_map/hyena_chain/pallas_call | solution.py:205
  106.8 0.7 copy.61
  107.6 3.3 %all-to-all-start.8 = ((f32[8,3,7,2]{2,3,1,0:T(2,128)}), f32[8,3,7,2]{2,3,1,0:T(2,128)S(1)}, u32[]{:S(2)}, u32[]{:S(2)}) async-start(f32[8,3,7,2]{2,3,1,0:T(2,128)} %copy.61), calls=%async_computation.8 | async-start | bytes 49152 | tf_op jit(solution)/shard_map/all_to_all | solution.py:253
  110.9 0.8 reshape.51
  111.7 4.6 %all-to-all-done.8 = f32[8,3,7,2]{2,3,1,0:T(2,128)S(1)} async-done(((f32[8,3,7,2]{2,3,1,0:T(2,128)}), f32[8,3,7,2]{2,3,1,0:T(2,128)S(1)}, u32[]{:S(2)}, u32[]{:S(2)}) %all-to-all-start.8) | async-done | bytes 1376 | tf_op jit(solution)/shard_map/all_to_all | solution.py:253
  116.2 3.4 %all-to-all-start.5 = ((bf16[8,2,8192]{2,1,0:T(2,128)(2,1)}), bf16[8,2,8192]{2,1,0:T(2,128)(2,1)S(1)}, u32[]{:S(2)}, u32[]{:S(2)}) async-start(bf16[8,2,8192]{2,1,0:T(2,128)(2,1)} %reshape.51), calls=%async_computation.5 | async-start | bytes 524288 | tf_op jit(solution)/shard_map/all_to_all | solution.py:254
  119.7 1.1 reshape.52
  120.7 6.4 %all-to-all-done.5 = bf16[8,2,8192]{2,1,0:T(2,128)(2,1)S(1)} async-done(((bf16[8,2,8192]{2,1,0:T(2,128)(2,1)}), bf16[8,2,8192]{2,1,0:T(2,128)(2,1)S(1)}, u32[]{:S(2)}, u32[]{:S(2)}) %all-to-all-start.5) | async-done | bytes 262176 | tf_op jit(solution)/shard_map/all_to_all | solution.py:254
  127.1 3.5 %all-to-all-start.7 = ((f32[8,2,8192]{2,1,0:T(2,128)}), f32[8,2,8192]{2,1,0:T(2,128)S(1)}, u32[]{:S(2)}, u32[]{:S(2)}) async-start(f32[8,2,8192]{2,1,0:T(2,128)} %reshape.52), calls=%async_computation.7 | async-start | bytes 1048576 | tf_op jit(solution)/shard_map/all_to_all | solution.py:252
  130.8 0.9 copy.59
  131.7 9.2 %all-to-all-done.7 = f32[8,2,8192]{2,1,0:T(2,128)S(1)} async-done(((f32[8,2,8192]{2,1,0:T(2,128)}), f32[8,2,8192]{2,1,0:T(2,128)S(1)}, u32[]{:S(2)}, u32[]{:S(2)}) %all-to-all-start.7) | async-done | bytes 524320 | tf_op jit(solution)/shard_map/all_to_all | solution.py:252
  140.9 5.1 %all-to-all-start.6 = ((bf16[16,64,128]{2,0,1:T(8,128)(2,1)}), bf16[16,64,128]{2,0,1:T(8,128)(2,1)S(1)}, u32[]{:S(2)}, u32[]{:S(2)}) async-start(bf16[16,64,128]{2,0,1:T(8,128)(2,1)} %copy.59), calls=%async_computation.6 | async-start | bytes 524288 | tf_op jit(solution)/shard_map/all_to_all | solution.py:255
  146.1 0.7 copy.63
  146.7 1.2 all_to_all.86
  147.9 12.7 %all-to-all-done.6 = bf16[16,64,128]{2,0,1:T(8,128)(2,1)S(1)} async-done(((bf16[16,64,128]{2,0,1:T(8,128)(2,1)}), bf16[16,64,128]{2,0,1:T(8,128)(2,1)S(1)}, u32[]{:S(2)}, u32[]{:S(2)}) %all-to-all-start.6) | async-done | bytes 262176 | tf_op jit(solution)/shard_map/all_to_all | solution.py:255
  160.5 0.7 copy.70
  (31 shorter events, 4.6 us)
Async XLA Ops:
  0.6 5.9 %copy-start = (bf16[1024,128]{1,0:T(8,128)(2,1)S(1)}, bf16[1024,128]{1,0:T(8,128)(2,1)}, u32[]{:S(2)}) copy-start(bf16[1024,128]{1,0:T(8,128)(2,1)} %param.5) | copy-start | bytes 786436
  0.6 27.9 %copy-start.1 = (bf16[1,1024,128]{2,1,0:T(8,128)(2,1)S(1)}, bf16[1,1024,128]{2,1,0:T(8,128)(2,1)}, u32[]{:S(2)}) copy-start(bf16[1,1024,128]{2,1,0:T(8,128)(2,1)} %param.4) | copy-start | bytes 786436
  2.2 9.7 %all-to-all-start = ((f32[8,3,7,2]{2,3,1,0:T(2,128)}), f32[8,3,7,2]{2,3,1,0:T(2,128)S(1)}, u32[]{:S(2)}, u32[]{:S(2)}) async-start(f32[8,3,7,2]{2,3,1,0:T(2,128)} %copy.53), calls=%async_computation | async-start | bytes 49152 | tf_op jit(solution)/shard_map/all_to_all | solution.py:246
  11.9 27.5 %all-to-all-start.4 = ((bf16[64,2,128]{2,1,0:T(2,128)(2,1)}), bf16[64,2,128]{2,1,0:T(2,128)(2,1)S(1)}, u32[]{:S(2)}, u32[]{:S(2)}) async-start(bf16[64,2,128]{2,1,0:T(2,128)(2,1)} %dynamic-slice_bitcast_fusion), calls=%async_computation.4 | async-start | bytes 65536 | tf_op jit(solution)/shard_map/all_to_all | solution.py:250
  32.4 12.8 %copy-start.2 = (bf16[1,16,8192]{2,1,0:T(8,128)(2,1)S(1)}, bf16[1,16,8192]{2,1,0:T(8,128)(2,1)}, u32[]{:S(2)}) copy-start(bf16[1,16,8192]{2,1,0:T(8,128)(2,1)} %param.6) | copy-start | bytes 786436
  39.5 19.5 %all-to-all-start.1 = ((bf16[64,2,1024]{2,1,0:T(2,128)(2,1)}), bf16[64,2,1024]{2,1,0:T(2,128)(2,1)S(1)}, u32[]{:S(2)}, u32[]{:S(2)}) async-start(bf16[64,2,1024]{2,1,0:T(2,128)(2,1)} %reshape.54), calls=%async_computation.1 | async-start | bytes 524288 | tf_op jit(solution)/shard_map/all_to_all | solution.py:237
  59.0 10.9 %all-to-all-start.3 = ((bf16[8,2,8192]{2,1,0:T(2,128)(2,1)}), bf16[8,2,8192]{2,1,0:T(2,128)(2,1)S(1)}, u32[]{:S(2)}, u32[]{:S(2)}) async-start(bf16[8,2,8192]{2,1,0:T(2,128)(2,1)} %reshape_squeeze.10), calls=%async_computation.3 | async-start | bytes 524288 | tf_op jit(solution)/shard_map/all_to_all | solution.py:241
  69.9 10.9 %all-to-all-start.2 = ((bf16[8,2,8192]{2,1,0:T(2,128)(2,1)}), bf16[8,2,8192]{2,1,0:T(2,128)(2,1)S(1)}, u32[]{:S(2)}, u32[]{:S(2)}) async-start(bf16[8,2,8192]{2,1,0:T(2,128)(2,1)} %reshape_squeeze.9), calls=%async_computation.2 | async-start | bytes 524288 | tf_op jit(solution)/shard_map/all_to_all | solution.py:238
  107.6 8.7 %all-to-all-start.8 = ((f32[8,3,7,2]{2,3,1,0:T(2,128)}), f32[8,3,7,2]{2,3,1,0:T(2,128)S(1)}, u32[]{:S(2)}, u32[]{:S(2)}) async-start(f32[8,3,7,2]{2,3,1,0:T(2,128)} %copy.61), calls=%async_computation.8 | async-start | bytes 49152 | tf_op jit(solution)/shard_map/all_to_all | solution.py:253
  116.2 10.9 %all-to-all-start.5 = ((bf16[8,2,8192]{2,1,0:T(2,128)(2,1)}), bf16[8,2,8192]{2,1,0:T(2,128)(2,1)S(1)}, u32[]{:S(2)}, u32[]{:S(2)}) async-start(bf16[8,2,8192]{2,1,0:T(2,128)(2,1)} %reshape.51), calls=%async_computation.5 | async-start | bytes 524288 | tf_op jit(solution)/shard_map/all_to_all | solution.py:254
  127.1 13.8 %all-to-all-start.7 = ((f32[8,2,8192]{2,1,0:T(2,128)}), f32[8,2,8192]{2,1,0:T(2,128)S(1)}, u32[]{:S(2)}, u32[]{:S(2)}) async-start(f32[8,2,8192]{2,1,0:T(2,128)} %reshape.52), calls=%async_computation.7 | async-start | bytes 1048576 | tf_op jit(solution)/shard_map/all_to_all | solution.py:252
  140.9 19.7 %all-to-all-start.6 = ((bf16[16,64,128]{2,0,1:T(8,128)(2,1)}), bf16[16,64,128]{2,0,1:T(8,128)(2,1)S(1)}, u32[]{:S(2)}, u32[]{:S(2)}) async-start(bf16[16,64,128]{2,0,1:T(8,128)(2,1)} %copy.59), calls=%async_computation.6 | async-start | bytes 524288 | tf_op jit(solution)/shard_map/all_to_all | solution.py:255
where the time goes:
time: 162 us; the launch traced here: 161 us
  waiting for transfers between devices  69.1 us (43%)
  starting transfers between devices  48.9 us (30%)
  Pallas kernels  25.6 us (16%)
  local copies, waits for them, and re-layouts  13 us (8%)
  other arithmetic  3.66 us (2%)
    pallas_call x1, Pallas kernels, run_chain(): pl.pallas_call(lambda *refs: chain_kernel(sub, *refs), out_shape=(jax.Sha...  25.6 us
    all_to_all x1, starting transfers between devices, shards(): og = lax.all_to_all(og, 'ctx', split_axis=0, concat_axis=2, tiled=True)[0]  16.6 us
    all_to_all x1, waiting for transfers between devices, shards(): ig = lax.all_to_all(ig, 'ctx', split_axis=1, concat_axis=0, tiled=True)  12.7 us
    all_to_all x1, waiting for transfers between devices, shards(): lax.all_to_all(inputs, 'ctx', split_axis=1, concat_axis=2, tiled=True)[0]  11.7 us
    all_to_all x1, waiting for transfers between devices, shards(): lax.all_to_all(filter_grad, 'section', split_axis=0, concat_axis=1, tiled...  9.18 us
    all_to_all x1, waiting for transfers between devices, shards(): og = lax.all_to_all(og, 'ctx', split_axis=0, concat_axis=2, tiled=True)[0]  7.03 us
    all_to_all x1, waiting for transfers between devices, shards(): lax.all_to_all(x_ctx.reshape(sec_n, sub, length), 'section', split_axis=0...  6.75 us
    all_to_all x1, waiting for transfers between devices, shards(): lax.all_to_all(in_all, 'section', split_axis=0, concat_axis=1, tiled=True)  6.36 us
  transfers between devices with their start and end apart: 9, of which 9 were waited for; matrix products, arithmetic and copies ran while one was open for 7% of the time, Pallas kernels for 0%

commit v1 on v0

--- a/solution.py
+++ b/solution.py
@@ -225,6 +225,22 @@
     return in_k.reshape(layers, sub, length), fg_k.reshape(layers, sub, length), tap_grad
 
 
+def exact_pieces(value):
+    pieces = []
+    rest = value
+    for _ in range(3):
+        high = lax.reduce_precision(rest, exponent_bits=8, mantissa_bits=7)
+        pieces.append(high.astype(jnp.bfloat16))
+        rest = rest - high
+    return jnp.concatenate(pieces, axis=-1)
+
+
+def joined(pieces):
+    third = pieces.shape[-1] // 3
+    parts = [pieces[..., i * third:(i + 1) * third].astype(jnp.float32) for i in range(3)]
+    return parts[0] + parts[1] + parts[2]
+
+
 def shards(inputs, out_grad, filters, conv_taps):
     sec_n = lax.axis_size("section")
     ctx_n = lax.axis_size("ctx")
@@ -234,24 +250,42 @@
     length = filters.shape[2]
     sub = channels // sec_n
     tok_dev = inputs.shape[2]
-    x_ctx = lax.all_to_all(inputs, "ctx", split_axis=1, concat_axis=2, tiled=True)[0]
-    x_all = lax.all_to_all(
-        x_ctx.reshape(sec_n, sub, length), "section", split_axis=0, concat_axis=0, tiled=True
-    )
-    h_all = lax.all_to_all(
-        filters[0].reshape(sec_n, sub, length), "section", split_axis=0, concat_axis=0, tiled=True
-    )
-    taps_c = lax.dynamic_slice_in_dim(conv_taps[0], ctx * channels, channels, 2)
-    taps_c = jnp.moveaxis(taps_c.reshape(3, 7, sec_n, sub), 2, 0)
-    taps_all = lax.all_to_all(taps_c, "section", split_axis=0, concat_axis=0, tiled=True)
+    span = sub * length
     og = lax.dynamic_index_in_dim(
         out_grad.reshape(ctx_n, sec_n, sub, tok_dev), sec, 1, keepdims=False
     )
-    og = lax.all_to_all(og, "ctx", split_axis=0, concat_axis=2, tiled=True)[0]
+    sent = jnp.concatenate([inputs[0].reshape(ctx_n, channels, tok_dev), og], axis=1)
+    got = lax.all_to_all(sent, "ctx", split_axis=0, concat_axis=2, tiled=True)[0]
+    x_ctx = got[:channels]
+    og = got[channels:]
+    taps_c = lax.dynamic_slice_in_dim(conv_taps[0], ctx * channels, channels, 2)
+    taps_c = jnp.moveaxis(taps_c.reshape(3, 7, sec_n, sub), 2, 0).reshape(sec_n, 21 * sub)
+    sent = jnp.concatenate(
+        [
+            x_ctx.reshape(sec_n, span),
+            filters[0].reshape(sec_n, span),
+            exact_pieces(taps_c),
+        ],
+        axis=1,
+    )
+    got = lax.all_to_all(sent, "section", split_axis=0, concat_axis=0, tiled=True)
+    x_all = got[:, :span].reshape(sec_n, sub, length)
+    h_all = got[:, span:2 * span].reshape(sec_n, sub, length)
+    taps_all = joined(got[:, 2 * span:]).reshape(sec_n, 3, 7, sub)
     in_all, filter_grad, tap_grad = run_chain(x_all, h_all, og, taps_all)
-    fg = lax.all_to_all(filter_grad, "section", split_axis=0, concat_axis=1, tiled=True)
-    tg = lax.all_to_all(tap_grad, "section", split_axis=0, concat_axis=3, tiled=True)
-    ig = lax.all_to_all(in_all, "section", split_axis=0, concat_axis=1, tiled=True)[0]
+    sent = jnp.concatenate(
+        [
+            filter_grad.reshape(sec_n, span),
+            in_all.reshape(sec_n, span).astype(jnp.float32),
+            tap_grad.reshape(sec_n, 21 * sub),
+        ],
+        axis=1,
+    )
+    got = lax.all_to_all(sent, "section", split_axis=0, concat_axis=0, tiled=True)
+    fg = got[:, :span].reshape(1, channels, length)
+    ig = got[:, span:2 * span].astype(jnp.bfloat16).reshape(channels, length)
+    tg = jnp.moveaxis(got[:, 2 * span:].reshape(sec_n, 3, 7, sub), 0, 2)
+    tg = tg.reshape(1, 3, 7, channels)
     ig = lax.all_to_all(ig, "ctx", split_axis=1, concat_axis=0, tiled=True)
     return (ig[None], fg, tg)
 

time: 162 us -> 126 us (0.78)
  waiting for transfers between devices: 69.1 us -> 37.7 us
  starting transfers between devices: 48.9 us -> 25.8 us
  blocking collectives: 0 us -> 18.6 us
    all_to_all x8 -> x2, waiting for transfers between devices: 56.5 us -> 24.6 us  [the longest x1 14.7 us: shards(): lax.all_to_all(sent, 'ctx', split_axis=0, concat_axis=2, tiled=True)[0]]
    all_to_all x8 -> x2, starting transfers between devices: 43.8 us -> 20.9 us  [the longest x1 16.6 us: shards(): lax.all_to_all(sent, 'ctx', split_axis=0, concat_axis=2, tiled=True)[0]]
    all_to_all x0 -> x1, blocking collectives: none -> 18.6 us  [shards(): lax.all_to_all(sent, 'section', split_axis=0, concat_axis=0, tiled=True)]
    unnamed x14 -> x18, local copies, waits for them, and re-layouts: 3.46 us -> 6.98 us
    unnamed x1, other arithmetic: 2.21 us -> 0.04 us
    reshape x7 -> x5, local copies, waits for them, and re-layouts: 3.15 us -> 1.1 us  [the longest x1 0.87 us: shards(): fg = got[:, :span].reshape(1, channels, length)]
    concatenate x0 -> x2, other arithmetic: none -> 1.81 us  [the longest x1 1.74 us: shards(): jnp.concatenate([inputs[0].reshape(ctx_n, channels, tok_dev), og], axis=1)]
  transfers between devices with their start and end apart: 9 -> 3, of which waited for: 9 -> 3; matrix products, arithmetic and copies ran while one was open for 7% -> 4% of each run, Pallas kernels for 0% -> 0%
where the time goes in v1:
time: 126 us; the launch traced here: 125 us
  waiting for transfers between devices  37.7 us (30%)
  starting transfers between devices  25.8 us (20%)
  Pallas kernels  25.7 us (20%)
  blocking collectives  18.6 us (15%)
  local copies, waits for them, and re-layouts  12.1 us (10%)
  other arithmetic  4.44 us (4%)
    pallas_call x1, Pallas kernels, run_chain(): pl.pallas_call(lambda *refs: chain_kernel(sub, *refs), out_shape=(jax.Sha...  25.7 us
    all_to_all x1, blocking collectives, shards(): lax.all_to_all(sent, 'section', split_axis=0, concat_axis=0, tiled=True)  18.6 us
    all_to_all x1, starting transfers between devices, shards(): lax.all_to_all(sent, 'ctx', split_axis=0, concat_axis=2, tiled=True)[0]  16.6 us
    all_to_all x1, waiting for transfers between devices, shards(): lax.all_to_all(sent, 'ctx', split_axis=0, concat_axis=2, tiled=True)[0]  14.7 us
    all_to_all x1, waiting for transfers between devices, shards(): ig = lax.all_to_all(ig, 'ctx', split_axis=1, concat_axis=0, tiled=True)  13 us
    all_to_all x1, waiting for transfers between devices, shards(): lax.all_to_all(sent, 'section', split_axis=0, concat_axis=0, tiled=True)  9.95 us
    unnamed x18, local copies, waits for them, and re-layouts  6.98 us
    all_to_all x1, starting transfers between devices, shards(): ig = lax.all_to_all(ig, 'ctx', split_axis=1, concat_axis=0, tiled=True)  4.94 us
  transfers between devices with their start and end apart: 3, of which 3 were waited for; matrix products, arithmetic and copies ran while one was open for 4% of the time, Pallas kernels for 0%

profile of v1, /device:TPU:8, one launch (start us, length us, event | category | flops | bytes accessed | tf_op | source)
XLA Modules:
  0.0 125.3 jit_solution(4584895350973669644)
XLA Ops:
  0.7 0.9 copy-done
  1.6 1.7 %pad_maximum_fusion.1 = bf16[64,18,128]{2,1,0:T(8,128)(2,1)} fusion(bf16[64,2,128]{2,1,0:T(2,128)(2,1)S(1)} %dynamic-slice_bitcast_fusion, bf16[64,16,128]{2,1,0:T(8,128)(2,1)} %bitcast.62), kind=kLoop, calls=%fused_computation.7 | loop fusion | flops 589824 | bytes 589824 | tf_op jit(solution)/shard_map/concatenate | solution.py:257
  3.4 16.6 %all-to-all-start = ((bf16[64,18,128]{2,1,0:T(8,128)(2,1)}), bf16[64,18,128]{2,1,0:T(8,128)(2,1)S(1)}, u32[]{:S(2)}, u32[]{:S(2)}) async-start(bf16[64,18,128]{2,1,0:T(8,128)(2,1)} %pad_maximum_fusion.1), calls=%async_computation | async-start | bytes 786432 | tf_op jit(solution)/shard_map/all_to_all | solution.py:258
  19.9 0.3 fusion.34
  20.2 0.8 constant_dynamic-slice_fusion
  21.1 0.1 copy.64
  21.4 0.1 sine_negate_fusion.1
  21.6 0.3 fusion.28
  21.9 0.3 sine_negate_fusion
  22.2 14.7 %all-to-all-done = bf16[64,18,128]{2,1,0:T(8,128)(2,1)S(1)} async-done(((bf16[64,18,128]{2,1,0:T(8,128)(2,1)}), bf16[64,18,128]{2,1,0:T(8,128)(2,1)S(1)}, u32[]{:S(2)}, u32[]{:S(2)}) %all-to-all-start) | async-done | bytes 294944 | tf_op jit(solution)/shard_map/all_to_all | solution.py:258
  37.1 0.1 dynamic-update-slice.2
  37.3 0.2 dynamic-update-slice.3
  37.5 0.2 dynamic-update-slice.4
  37.7 0.5 broadcast.51
  38.2 1.1 reduce
  39.3 1.2 reshape.58
  40.5 4.3 %all-to-all-start.1 = ((bf16[8,2,16447]{2,1,0:T(2,128)(2,1)}), bf16[8,2,16447]{2,1,0:T(2,128)(2,1)S(1)}, u32[]{:S(2)}, u32[]{:S(2)}) async-start(bf16[8,2,16447]{2,1,0:T(2,128)(2,1)} %reshape.58), calls=%async_computation.1 | async-start | bytes 1056768 | tf_op jit(solution)/shard_map/all_to_all | solution.py:271
  44.8 0.3 fusion.30
  45.2 10.0 %all-to-all-done.1 = bf16[8,2,16447]{2,1,0:T(2,128)(2,1)S(1)} async-done(((bf16[8,2,16447]{2,1,0:T(2,128)(2,1)}), bf16[8,2,16447]{2,1,0:T(2,128)(2,1)S(1)}, u32[]{:S(2)}, u32[]{:S(2)}) %all-to-all-start.1) | async-done | bytes 526336 | tf_op jit(solution)/shard_map/all_to_all | solution.py:271
  55.2 2.2 %reshape.59 = bf16[8,1,32894]{2,1,0:T(2,128)(2,1)S(1)} reshape(bf16[8,2,16447]{2,1,0:T(2,128)(2,1)S(1)} %all-to-all-done.1) | data formatting | bytes 1052608
  57.7 25.7 %hyena_chain.1 = (bf16[8,128,128]{2,1,0:T(8,128)(2,1)S(1)}, f32[8,128,128]{2,1,0:T(8,128)S(1)}, f32[8,42,128]{2,1,0:T(8,128)S(1)}) custom-call(f32[336]{0:T(512)S(1)} %reshape_reshape.13.refs_0_, bf16[8,128,128]{2,1,0:T(8,128)(2,1)S(1)} %get-tuple-element.38.refs_1_, bf16[8,128,128]{2,1,0:T(8,128)(2,1)S(1)} %get-tuple-element.37.refs_2_, ...), custom_call_target="tpu_custom_call" | custom-call | tf_op jit(solution)/shard_map/hyena_chain/pallas_call | solution.py:205
  83.4 0.3 copy.89
  83.8 0.3 copy.90
  84.3 0.7 all_to_all.45
  85.0 18.6 %all_to_all.55 = f32[8,1,32810]{2,1,0:T(1,128)S(1)} all-to-all(f32[8,1,32810]{2,1,0:T(1,128)S(1)} %all_to_all.45), channel_id=1, replica_groups=mesh['section'=8,'ctx'=64] {'section'}, dimensions={0} | all-to-all | bytes 2099840 | tf_op jit(solution)/shard_map/all_to_all | solution.py:284
  103.7 0.1 all_to_all.48
  103.9 0.9 copy.69
  104.7 4.9 %all-to-all-start.3 = ((bf16[16,64,128]{2,0,1:T(8,128)(2,1)}), bf16[16,64,128]{2,0,1:T(8,128)(2,1)S(1)}, u32[]{:S(2)}, u32[]{:S(2)}) async-start(bf16[16,64,128]{2,0,1:T(8,128)(2,1)} %copy.69), calls=%async_computation.3 | async-start | bytes 524288 | tf_op jit(solution)/shard_map/all_to_all | solution.py:289
  109.8 0.9 reshape.54
  110.9 0.7 copy.72
  111.5 13.0 %all-to-all-done.3 = bf16[16,64,128]{2,0,1:T(8,128)(2,1)S(1)} async-done(((bf16[16,64,128]{2,0,1:T(8,128)(2,1)}), bf16[16,64,128]{2,0,1:T(8,128)(2,1)S(1)}, u32[]{:S(2)}, u32[]{:S(2)}) %all-to-all-start.3) | async-done | bytes 262176 | tf_op jit(solution)/shard_map/all_to_all | solution.py:289
  124.6 0.7 copy.97
  (34 shorter events, 1.6 us)
Async XLA Ops:
  0.6 1.0 copy-start
  0.6 20.7 %copy-start.1 = (bf16[1,16,8192]{2,1,0:T(8,128)(2,1)S(1)}, bf16[1,16,8192]{2,1,0:T(8,128)(2,1)}, u32[]{:S(2)}) copy-start(bf16[1,16,8192]{2,1,0:T(8,128)(2,1)} %param.6) | copy-start | bytes 786436
  3.4 33.5 %all-to-all-start = ((bf16[64,18,128]{2,1,0:T(8,128)(2,1)}), bf16[64,18,128]{2,1,0:T(8,128)(2,1)S(1)}, u32[]{:S(2)}, u32[]{:S(2)}) async-start(bf16[64,18,128]{2,1,0:T(8,128)(2,1)} %pad_maximum_fusion.1), calls=%async_computation | async-start | bytes 786432 | tf_op jit(solution)/shard_map/all_to_all | solution.py:258
  40.5 14.7 %all-to-all-start.1 = ((bf16[8,2,16447]{2,1,0:T(2,128)(2,1)}), bf16[8,2,16447]{2,1,0:T(2,128)(2,1)S(1)}, u32[]{:S(2)}, u32[]{:S(2)}) async-start(bf16[8,2,16447]{2,1,0:T(2,128)(2,1)} %reshape.58), calls=%async_computation.1 | async-start | bytes 1056768 | tf_op jit(solution)/shard_map/all_to_all | solution.py:271
  104.7 19.8 %all-to-all-start.3 = ((bf16[16,64,128]{2,0,1:T(8,128)(2,1)}), bf16[16,64,128]{2,0,1:T(8,128)(2,1)S(1)}, u32[]{:S(2)}, u32[]{:S(2)}) async-start(bf16[16,64,128]{2,0,1:T(8,128)(2,1)} %copy.69), calls=%async_computation.3 | async-start | bytes 524288 | tf_op jit(solution)/shard_map/all_to_all | solution.py:289

commit v2 on v1

--- a/solution.py
+++ b/solution.py
@@ -194,9 +194,10 @@
 
 
 def run_chain(x_all, h_all, og, taps_all):
-    layers, sub, length = x_all.shape
-    half = length // LANES
-    rows = sub * half
+    layers, rows, _ = x_all.shape
+    sub = taps_all.shape[3]
+    half = rows // sub
+    length = half * LANES
     blocks = 2 * half
     tables = spectrum_tables(length)
     vmem = pl.BlockSpec(memory_space=pltpu.VMEM)
@@ -216,8 +217,8 @@
         name="hyena_chain",
     )(
         taps_all.reshape(-1),
-        x_all.reshape(layers, rows, LANES),
-        h_all.reshape(layers, rows, LANES),
+        x_all,
+        h_all,
         og.reshape(rows, LANES),
         *tables,
     )
@@ -258,33 +259,34 @@
     got = lax.all_to_all(sent, "ctx", split_axis=0, concat_axis=2, tiled=True)[0]
     x_ctx = got[:channels]
     og = got[channels:]
+    rows = sub * length // LANES
     taps_c = lax.dynamic_slice_in_dim(conv_taps[0], ctx * channels, channels, 2)
     taps_c = jnp.moveaxis(taps_c.reshape(3, 7, sec_n, sub), 2, 0).reshape(sec_n, 21 * sub)
+    taps_c = exact_pieces(taps_c)
+    taps_c = jnp.pad(taps_c, ((0, 0), (0, LANES - taps_c.shape[1])))
     sent = jnp.concatenate(
         [
-            x_ctx.reshape(sec_n, span),
-            filters[0].reshape(sec_n, span),
-            exact_pieces(taps_c),
+            x_ctx.reshape(sec_n, rows, LANES),
+            filters[0].reshape(sec_n, rows, LANES),
+            taps_c[:, None, :],
         ],
         axis=1,
     )
     got = lax.all_to_all(sent, "section", split_axis=0, concat_axis=0, tiled=True)
-    x_all = got[:, :span].reshape(sec_n, sub, length)
-    h_all = got[:, span:2 * span].reshape(sec_n, sub, length)
-    taps_all = joined(got[:, 2 * span:]).reshape(sec_n, 3, 7, sub)
+    x_all = got[:, :rows]
+    h_all = got[:, rows:2 * rows]
+    taps_all = joined(got[:, 2 * rows, :63 * sub]).reshape(sec_n, 3, 7, sub)
     in_all, filter_grad, tap_grad = run_chain(x_all, h_all, og, taps_all)
+    fg_high, fg_low = split_table(filter_grad.reshape(sec_n, span))
     sent = jnp.concatenate(
-        [
-            filter_grad.reshape(sec_n, span),
-            in_all.reshape(sec_n, span).astype(jnp.float32),
-            tap_grad.reshape(sec_n, 21 * sub),
-        ],
+        [fg_high, fg_low, in_all.reshape(sec_n, span), exact_pieces(tap_grad.reshape(sec_n, 21 * sub))],
         axis=1,
     )
     got = lax.all_to_all(sent, "section", split_axis=0, concat_axis=0, tiled=True)
-    fg = got[:, :span].reshape(1, channels, length)
-    ig = got[:, span:2 * span].astype(jnp.bfloat16).reshape(channels, length)
-    tg = jnp.moveaxis(got[:, 2 * span:].reshape(sec_n, 3, 7, sub), 0, 2)
+    fg = got[:, :span].astype(jnp.float32) + got[:, span:2 * span].astype(jnp.float32)
+    fg = fg.reshape(1, channels, length)
+    ig = got[:, 2 * span:3 * span].reshape(channels, length)
+    tg = jnp.moveaxis(joined(got[:, 3 * span:]).reshape(sec_n, 3, 7, sub), 0, 2)
     tg = tg.reshape(1, 3, 7, channels)
     ig = lax.all_to_all(ig, "ctx", split_axis=1, concat_axis=0, tiled=True)
     return (ig[None], fg, tg)

time: 126 us -> 123 us (0.976)
  blocking collectives: 18.6 us -> 15.8 us
  other arithmetic: 4.44 us -> 6.21 us
    all_to_all x1, blocking collectives: 18.6 us -> 15.8 us  [shards(): lax.all_to_all(sent, 'section', split_axis=0, concat_axis=0, tiled=True)]
    unnamed x18 -> x14, local copies, waits for them, and re-layouts: 6.98 us -> 6.77 us
where the time goes in v2:
time: 123 us
  waiting for transfers between devices  37.6 us (31%)
  starting transfers between devices  25.9 us (21%)
  Pallas kernels  25.6 us (21%)
  blocking collectives  15.8 us (13%)
  local copies, waits for them, and re-layouts  11 us (9%)
  other arithmetic  6.21 us (5%)
    pallas_call x1, Pallas kernels, run_chain(): pl.pallas_call(lambda *refs: chain_kernel(sub, *refs), out_shape=(jax.Sha...  25.6 us
    all_to_all x1, starting transfers between devices, shards(): lax.all_to_all(sent, 'ctx', split_axis=0, concat_axis=2, tiled=True)[0]  16.6 us
    all_to_all x1, blocking collectives, shards(): lax.all_to_all(sent, 'section', split_axis=0, concat_axis=0, tiled=True)  15.8 us
    all_to_all x1, waiting for transfers between devices, shards(): lax.all_to_all(sent, 'ctx', split_axis=0, concat_axis=2, tiled=True)[0]  14.6 us
    all_to_all x1, waiting for transfers between devices, shards(): ig = lax.all_to_all(ig, 'ctx', split_axis=1, concat_axis=0, tiled=True)  13 us
    all_to_all x1, waiting for transfers between devices, shards(): lax.all_to_all(sent, 'section', split_axis=0, concat_axis=0, tiled=True)  10.1 us
    unnamed x14, local copies, waits for them, and re-layouts  6.77 us
    all_to_all x1, starting transfers between devices, shards(): ig = lax.all_to_all(ig, 'ctx', split_axis=1, concat_axis=0, tiled=True)  4.97 us
  transfers between devices with their start and end apart: 3, of which 3 were waited for; matrix products, arithmetic and copies ran while one was open for 4% of the time, Pallas kernels for 0%

profile of v2, /device:TPU:8, one launch (start us, length us, event | category | flops | bytes accessed | tf_op | source)
XLA Modules:
  0.0 123.0 jit_solution(18360636752080897278)
XLA Ops:
  0.7 0.9 copy-done
  1.6 1.7 %pad_maximum_fusion.1 = bf16[64,18,128]{2,1,0:T(8,128)(2,1)} fusion(bf16[64,2,128]{2,1,0:T(2,128)(2,1)S(1)} %dynamic-slice_bitcast_fusion, bf16[64,16,128]{2,1,0:T(8,128)(2,1)} %bitcast.56), kind=kLoop, calls=%fused_computation.6 | loop fusion | flops 589824 | bytes 589824 | tf_op jit(solution)/shard_map/concatenate | solution.py:258
  3.4 16.6 %all-to-all-start = ((bf16[64,18,128]{2,1,0:T(8,128)(2,1)}), bf16[64,18,128]{2,1,0:T(8,128)(2,1)S(1)}, u32[]{:S(2)}, u32[]{:S(2)}) async-start(bf16[64,18,128]{2,1,0:T(8,128)(2,1)} %pad_maximum_fusion.1), calls=%async_computation | async-start | bytes 786432 | tf_op jit(solution)/shard_map/all_to_all | solution.py:259
  19.9 0.8 constant_dynamic-slice_fusion
  21.2 0.1 reshape_squeeze.7
  21.3 0.3 fusion.37
  21.6 0.1 sine_negate_fusion.1
  21.7 0.3 fusion.33
  22.0 0.3 fusion.31
  22.3 14.6 %all-to-all-done = bf16[64,18,128]{2,1,0:T(8,128)(2,1)S(1)} async-done(((bf16[64,18,128]{2,1,0:T(8,128)(2,1)}), bf16[64,18,128]{2,1,0:T(8,128)(2,1)S(1)}, u32[]{:S(2)}, u32[]{:S(2)}) %all-to-all-start) | async-done | bytes 294944 | tf_op jit(solution)/shard_map/all_to_all | solution.py:259
  36.9 0.8 pad_maximum_fusion
  37.8 4.3 %all-to-all-start.1 = ((bf16[8,257,128]{2,1,0:T(8,128)(2,1)}), bf16[8,257,128]{2,1,0:T(8,128)(2,1)S(1)}, u32[]{:S(2)}, u32[]{:S(2)}) async-start(bf16[8,257,128]{2,1,0:T(8,128)(2,1)} %pad_maximum_fusion), calls=%async_computation.1 | async-start | bytes 1081344 | tf_op jit(solution)/shard_map/all_to_all | solution.py:275
  42.1 0.3 sine_negate_fusion
  42.5 10.1 %all-to-all-done.1 = bf16[8,257,128]{2,1,0:T(8,128)(2,1)S(1)} async-done(((bf16[8,257,128]{2,1,0:T(8,128)(2,1)}), bf16[8,257,128]{2,1,0:T(8,128)(2,1)S(1)}, u32[]{:S(2)}, u32[]{:S(2)}) %all-to-all-start.1) | async-done | bytes 526368 | tf_op jit(solution)/shard_map/all_to_all | solution.py:275
  52.8 25.6 %hyena_chain.1 = (bf16[8,128,128]{2,1,0:T(8,128)(2,1)S(1)}, f32[8,128,128]{2,1,0:T(8,128)S(1)}, f32[8,42,128]{2,1,0:T(8,128)S(1)}) custom-call(f32[336]{0:T(512)S(1)} %reshape_reshape.9.refs_0_, bf16[8,128,128]{2,1,0:T(8,128)(2,1)S(1)} %get-tuple-element.28.refs_1_, bf16[8,128,128]{2,1,0:T(8,128)(2,1)S(1)} %get-tuple-element.27.refs_2_, ...), custom_call_target="tpu_custom_call" | custom-call | tf_op jit(solution)/shard_map/hyena_chain/pallas_call | solution.py:206
  78.6 0.3 fusion.6
  78.9 0.3 fusion.5
  79.2 0.2 bitcast_dynamic-update-slice_fusion
  79.4 0.1 dynamic-update-slice.3
  79.5 0.2 dynamic-update-slice.4
  79.8 0.2 dynamic-update-slice.5
  80.0 0.5 broadcast.61
  80.5 1.3 %reduce = bf16[8,49278]{1,0:T(8,128)(2,1)S(1)} reduce(bf16[8,1,49278]{2,0,1:T(8,128)(2,1)S(1)} %bitcast.51, bf16[]{:T(256)} %broadcast.61), dimensions={1}, to_apply=%copy.85.reduce_sub_computation | reduce | bytes 1576898 | tf_op jit(solution)/shard_map/all_to_all | solution.py:285
  81.8 0.5 reshape.53
  82.4 15.8 %all_to_all.48 = bf16[8,2,24639]{2,1,0:T(2,128)(2,1)S(1)} all-to-all(bf16[8,2,24639]{2,1,0:T(2,128)(2,1)S(1)} %reshape.53), channel_id=1, replica_groups=mesh['section'=8,'ctx'=64] {'section'}, dimensions={0} | all-to-all | bytes 1576896 | tf_op jit(solution)/shard_map/all_to_all | solution.py:285
  98.1 3.2 %reshape.54 = bf16[8,1,49278]{2,1,0:T(2,128)(2,1)S(1)} reshape(bf16[8,2,24639]{2,1,0:T(2,128)(2,1)S(1)} %all_to_all.48) | data formatting | bytes 1576896
  101.5 0.9 copy.86
  102.4 5.0 %all-to-all-start.3 = ((bf16[16,64,128]{2,0,1:T(8,128)(2,1)}), bf16[16,64,128]{2,0,1:T(8,128)(2,1)S(1)}, u32[]{:S(2)}, u32[]{:S(2)}) async-start(bf16[16,64,128]{2,0,1:T(8,128)(2,1)} %copy.86), calls=%async_computation.3 | async-start | bytes 524288 | tf_op jit(solution)/shard_map/all_to_all | solution.py:291
  107.8 0.7 copy.89
  108.5 0.9 reshape.50
  109.3 13.0 %all-to-all-done.3 = bf16[16,64,128]{2,0,1:T(8,128)(2,1)S(1)} async-done(((bf16[16,64,128]{2,0,1:T(8,128)(2,1)}), bf16[16,64,128]{2,0,1:T(8,128)(2,1)S(1)}, u32[]{:S(2)}, u32[]{:S(2)}) %all-to-all-start.3) | async-done | bytes 262176 | tf_op jit(solution)/shard_map/all_to_all | solution.py:291
  122.3 0.7 copy.114
  (33 shorter events, 1.6 us)
Async XLA Ops:
  0.6 1.0 copy-start
  0.6 20.5 %copy-start.1 = (bf16[1,16,8192]{2,1,0:T(8,128)(2,1)S(1)}, bf16[1,16,8192]{2,1,0:T(8,128)(2,1)}, u32[]{:S(2)}) copy-start(bf16[1,16,8192]{2,1,0:T(8,128)(2,1)} %param.6) | copy-start | bytes 786436
  3.4 33.5 %all-to-all-start = ((bf16[64,18,128]{2,1,0:T(8,128)(2,1)}), bf16[64,18,128]{2,1,0:T(8,128)(2,1)S(1)}, u32[]{:S(2)}, u32[]{:S(2)}) async-start(bf16[64,18,128]{2,1,0:T(8,128)(2,1)} %pad_maximum_fusion.1), calls=%async_computation | async-start | bytes 786432 | tf_op jit(solution)/shard_map/all_to_all | solution.py:259
  37.8 14.8 %all-to-all-start.1 = ((bf16[8,257,128]{2,1,0:T(8,128)(2,1)}), bf16[8,257,128]{2,1,0:T(8,128)(2,1)S(1)}, u32[]{:S(2)}, u32[]{:S(2)}) async-start(bf16[8,257,128]{2,1,0:T(8,128)(2,1)} %pad_maximum_fusion), calls=%async_computation.1 | async-start | bytes 1081344 | tf_op jit(solution)/shard_map/all_to_all | solution.py:275
  102.4 19.9 %all-to-all-start.3 = ((bf16[16,64,128]{2,0,1:T(8,128)(2,1)}), bf16[16,64,128]{2,0,1:T(8,128)(2,1)S(1)}, u32[]{:S(2)}, u32[]{:S(2)}) async-start(bf16[16,64,128]{2,0,1:T(8,128)(2,1)} %copy.86), calls=%async_computation.3 | async-start | bytes 524288 | tf_op jit(solution)/shard_map/all_to_all | solution.py:291

commit v3 on v2

--- a/solution.py
+++ b/solution.py
@@ -165,10 +165,10 @@
         grads = (grad_q, grad_w * v_s[layer], grad_w * k_s[layer])
         summed = jnp.zeros((rows, lanes), jnp.float32)
         for j in range(7):
-            term = tap(layer, 0, j) * ahead(grads[0], j)
-            term = term + tap(layer, 1, j) * ahead(grads[1], j)
-            term = term + tap(layer, 2, j) * ahead(grads[2], j)
-            summed = summed + term
+            term = tap(layer, 0, j) * grads[0]
+            term = term + tap(layer, 1, j) * grads[1]
+            term = term + tap(layer, 2, j) * grads[2]
+            summed = summed + ahead(term, j)
         rounded = summed.astype(jnp.bfloat16)
         in_ref[layer] = rounded
         x = x_ref[layer].astype(jnp.float32)
@@ -178,8 +178,10 @@
                 prod = grads[i] * xs
                 for c in range(sub):
                     row = (i * 7 + j) * sub + c
-                    part = jnp.sum(prod[c * half:(c + 1) * half, :], axis=0, keepdims=True)
-                    tp_ref[layer, pl.ds(row, 1), :] = part
+                    part = prod[c * half:c * half + 8, :]
+                    for r in range(c * half + 8, (c + 1) * half, 8):
+                        part = part + prod[r:r + 8, :]
+                    tp_ref[layer, row] = part
         return rounded.astype(jnp.float32)
 
     lax.fori_loop(0, layers, phase_two, og_ref[...].astype(jnp.float32))
@@ -208,7 +210,7 @@
         out_shape=(
             jax.ShapeDtypeStruct((layers, rows, LANES), jnp.bfloat16),
             jax.ShapeDtypeStruct((layers, rows, LANES), jnp.float32),
-            jax.ShapeDtypeStruct((layers, 21 * sub, LANES), jnp.float32),
+            jax.ShapeDtypeStruct((layers, 21 * sub, 8, LANES), jnp.float32),
         ),
         in_specs=[pl.BlockSpec(memory_space=pltpu.SMEM)] + [vmem] * 13,
         out_specs=(vmem, vmem, vmem),
@@ -222,7 +224,7 @@
         og.reshape(rows, LANES),
         *tables,
     )
-    tap_grad = jnp.sum(tp_k, axis=2).reshape(layers, 3, 7, sub)
+    tap_grad = jnp.sum(tp_k, axis=(2, 3)).reshape(layers, 3, 7, sub)
     return in_k.reshape(layers, sub, length), fg_k.reshape(layers, sub, length), tap_grad
 
 

time: 123 us -> 123 us (level)
  no operation moved by 1% of the time
where the time goes in v3:
time: 123 us; the launch traced here: 122 us
  waiting for transfers between devices  37.6 us (31%)
  starting transfers between devices  25.8 us (21%)
  Pallas kernels  24.6 us (20%)
  blocking collectives  15.8 us (13%)
  local copies, waits for them, and re-layouts  11 us (9%)
  other arithmetic  6.66 us (5%)
    pallas_call x1, Pallas kernels, run_chain(): pl.pallas_call(lambda *refs: chain_kernel(sub, *refs), out_shape=(jax.Sha...  24.6 us
    all_to_all x1, starting transfers between devices, shards(): lax.all_to_all(sent, 'ctx', split_axis=0, concat_axis=2, tiled=True)[0]  16.6 us
    all_to_all x1, blocking collectives, shards(): lax.all_to_all(sent, 'section', split_axis=0, concat_axis=0, tiled=True)  15.8 us
    all_to_all x1, waiting for transfers between devices, shards(): lax.all_to_all(sent, 'ctx', split_axis=0, concat_axis=2, tiled=True)[0]  14.6 us
    all_to_all x1, waiting for transfers between devices, shards(): ig = lax.all_to_all(ig, 'ctx', split_axis=1, concat_axis=0, tiled=True)  13 us
    all_to_all x1, waiting for transfers between devices, shards(): lax.all_to_all(sent, 'section', split_axis=0, concat_axis=0, tiled=True)  10.1 us
    unnamed x14, local copies, waits for them, and re-layouts  6.77 us
    all_to_all x1, starting transfers between devices, shards(): ig = lax.all_to_all(ig, 'ctx', split_axis=1, concat_axis=0, tiled=True)  4.96 us
  transfers between devices with their start and end apart: 3, of which 3 were waited for; matrix products, arithmetic and copies ran while one was open for 4% of the time, Pallas kernels for 0%

profile of v3, /device:TPU:8, one launch (start us, length us, event | category | flops | bytes accessed | tf_op | source)
XLA Modules:
  0.0 122.4 jit_solution(10807729702469743237)
XLA Ops:
  0.7 0.9 copy-done
  1.6 1.7 %pad_maximum_fusion.1 = bf16[64,18,128]{2,1,0:T(8,128)(2,1)} fusion(bf16[64,2,128]{2,1,0:T(2,128)(2,1)S(1)} %dynamic-slice_bitcast_fusion, bf16[64,16,128]{2,1,0:T(8,128)(2,1)} %bitcast.56), kind=kLoop, calls=%fused_computation.6 | loop fusion | flops 589824 | bytes 589824 | tf_op jit(solution)/shard_map/concatenate | solution.py:260
  3.4 16.6 %all-to-all-start = ((bf16[64,18,128]{2,1,0:T(8,128)(2,1)}), bf16[64,18,128]{2,1,0:T(8,128)(2,1)S(1)}, u32[]{:S(2)}, u32[]{:S(2)}) async-start(bf16[64,18,128]{2,1,0:T(8,128)(2,1)} %pad_maximum_fusion.1), calls=%async_computation | async-start | bytes 786432 | tf_op jit(solution)/shard_map/all_to_all | solution.py:261
  20.0 0.8 constant_dynamic-slice_fusion
  21.3 0.3 fusion.37
  21.6 0.1 sine_negate_fusion.1
  21.7 0.3 fusion.33
  22.0 0.3 fusion.31
  22.3 14.6 %all-to-all-done = bf16[64,18,128]{2,1,0:T(8,128)(2,1)S(1)} async-done(((bf16[64,18,128]{2,1,0:T(8,128)(2,1)}), bf16[64,18,128]{2,1,0:T(8,128)(2,1)S(1)}, u32[]{:S(2)}, u32[]{:S(2)}) %all-to-all-start) | async-done | bytes 294944 | tf_op jit(solution)/shard_map/all_to_all | solution.py:261
  36.9 0.8 pad_maximum_fusion
  37.8 4.3 %all-to-all-start.1 = ((bf16[8,257,128]{2,1,0:T(8,128)(2,1)}), bf16[8,257,128]{2,1,0:T(8,128)(2,1)S(1)}, u32[]{:S(2)}, u32[]{:S(2)}) async-start(bf16[8,257,128]{2,1,0:T(8,128)(2,1)} %pad_maximum_fusion), calls=%async_computation.1 | async-start | bytes 1081344 | tf_op jit(solution)/shard_map/all_to_all | solution.py:277
  42.1 0.3 sine_negate_fusion
  42.5 10.1 %all-to-all-done.1 = bf16[8,257,128]{2,1,0:T(8,128)(2,1)S(1)} async-done(((bf16[8,257,128]{2,1,0:T(8,128)(2,1)}), bf16[8,257,128]{2,1,0:T(8,128)(2,1)S(1)}, u32[]{:S(2)}, u32[]{:S(2)}) %all-to-all-start.1) | async-done | bytes 526368 | tf_op jit(solution)/shard_map/all_to_all | solution.py:277
  52.8 24.6 %hyena_chain.1 = (bf16[8,128,128]{2,1,0:T(8,128)(2,1)S(1)}, f32[8,128,128]{2,1,0:T(8,128)S(1)}, f32[8,42,8,128]{3,2,1,0:T(8,128)S(1)}) custom-call(f32[336]{0:T(512)S(1)} %reshape_reshape.9.refs_0_, bf16[8,128,128]{2,1,0:T(8,128)(2,1)S(1)} %get-tuple-element.28.refs_1_, bf16[8,128,128]{2,1,0:T(8,128)(2,1)S(1)} %get-tuple-element.27.refs_2_, ...), custom_call_target="tpu_custom_call" | custom-call | tf_op jit(solution)/shard_map/hyena_chain/pallas_call | solution.py:208
  77.4 0.6 reduce_sum.9
  78.0 0.3 fusion.6
  78.3 0.3 fusion.5
  78.6 0.2 bitcast_dynamic-update-slice_fusion
  78.8 0.1 dynamic-update-slice.3
  78.9 0.2 dynamic-update-slice.4
  79.2 0.2 dynamic-update-slice.5
  79.4 0.5 broadcast.61
  79.9 1.3 %reduce = bf16[8,49278]{1,0:T(8,128)(2,1)S(1)} reduce(bf16[8,1,49278]{2,0,1:T(8,128)(2,1)S(1)} %bitcast.51, bf16[]{:T(256)} %broadcast.61), dimensions={1}, to_apply=%copy.85.reduce_sub_computation | reduce | bytes 1576898 | tf_op jit(solution)/shard_map/all_to_all | solution.py:287
  81.2 0.5 reshape.53
  81.7 15.8 %all_to_all.48 = bf16[8,2,24639]{2,1,0:T(2,128)(2,1)S(1)} all-to-all(bf16[8,2,24639]{2,1,0:T(2,128)(2,1)S(1)} %reshape.53), channel_id=1, replica_groups=mesh['section'=8,'ctx'=64] {'section'}, dimensions={0} | all-to-all | bytes 1576896 | tf_op jit(solution)/shard_map/all_to_all | solution.py:287
  97.5 3.2 %reshape.54 = bf16[8,1,49278]{2,1,0:T(2,128)(2,1)S(1)} reshape(bf16[8,2,24639]{2,1,0:T(2,128)(2,1)S(1)} %all_to_all.48) | data formatting | bytes 1576896
  100.9 0.9 copy.86
  101.8 5.0 %all-to-all-start.3 = ((bf16[16,64,128]{2,0,1:T(8,128)(2,1)}), bf16[16,64,128]{2,0,1:T(8,128)(2,1)S(1)}, u32[]{:S(2)}, u32[]{:S(2)}) async-start(bf16[16,64,128]{2,0,1:T(8,128)(2,1)} %copy.86), calls=%async_computation.3 | async-start | bytes 524288 | tf_op jit(solution)/shard_map/all_to_all | solution.py:293
  107.2 0.7 copy.89
  107.8 0.9 reshape.50
  108.7 13.0 %all-to-all-done.3 = bf16[16,64,128]{2,0,1:T(8,128)(2,1)S(1)} async-done(((bf16[16,64,128]{2,0,1:T(8,128)(2,1)}), bf16[16,64,128]{2,0,1:T(8,128)(2,1)S(1)}, u32[]{:S(2)}, u32[]{:S(2)}) %all-to-all-start.3) | async-done | bytes 262176 | tf_op jit(solution)/shard_map/all_to_all | solution.py:293
  121.7 0.7 copy.114
  (33 shorter events, 1.6 us)
Async XLA Ops:
  0.6 1.0 copy-start
  0.6 20.5 %copy-start.1 = (bf16[1,16,8192]{2,1,0:T(8,128)(2,1)S(1)}, bf16[1,16,8192]{2,1,0:T(8,128)(2,1)}, u32[]{:S(2)}) copy-start(bf16[1,16,8192]{2,1,0:T(8,128)(2,1)} %param.6) | copy-start | bytes 786436
  3.4 33.5 %all-to-all-start = ((bf16[64,18,128]{2,1,0:T(8,128)(2,1)}), bf16[64,18,128]{2,1,0:T(8,128)(2,1)S(1)}, u32[]{:S(2)}, u32[]{:S(2)}) async-start(bf16[64,18,128]{2,1,0:T(8,128)(2,1)} %pad_maximum_fusion.1), calls=%async_computation | async-start | bytes 786432 | tf_op jit(solution)/shard_map/all_to_all | solution.py:261
  37.8 14.8 %all-to-all-start.1 = ((bf16[8,257,128]{2,1,0:T(8,128)(2,1)}), bf16[8,257,128]{2,1,0:T(8,128)(2,1)S(1)}, u32[]{:S(2)}, u32[]{:S(2)}) async-start(bf16[8,257,128]{2,1,0:T(8,128)(2,1)} %pad_maximum_fusion), calls=%async_computation.1 | async-start | bytes 1081344 | tf_op jit(solution)/shard_map/all_to_all | solution.py:277
  101.8 19.9 %all-to-all-start.3 = ((bf16[16,64,128]{2,0,1:T(8,128)(2,1)}), bf16[16,64,128]{2,0,1:T(8,128)(2,1)S(1)}, u32[]{:S(2)}, u32[]{:S(2)}) async-start(bf16[16,64,128]{2,0,1:T(8,128)(2,1)} %copy.86), calls=%async_computation.3 | async-start | bytes 524288 | tf_op jit(solution)/shard_map/all_to_all | solution.py:293

commit v4 on v3

--- a/solution.py
+++ b/solution.py
@@ -280,15 +280,19 @@
     taps_all = joined(got[:, 2 * rows, :63 * sub]).reshape(sec_n, 3, 7, sub)
     in_all, filter_grad, tap_grad = run_chain(x_all, h_all, og, taps_all)
     fg_high, fg_low = split_table(filter_grad.reshape(sec_n, span))
+    taps_out = exact_pieces(tap_grad.reshape(sec_n, 21 * sub))
+    taps_out = jnp.pad(taps_out, ((0, 0), (0, LANES - taps_out.shape[1])))
     sent = jnp.concatenate(
-        [fg_high, fg_low, in_all.reshape(sec_n, span), exact_pieces(tap_grad.reshape(sec_n, 21 * sub))],
+        [fg_high, fg_low, in_all.reshape(sec_n, span), taps_out],
         axis=1,
     )
-    got = lax.all_to_all(sent, "section", split_axis=0, concat_axis=0, tiled=True)
+    got = lax.all_to_all(
+        sent.reshape(sec_n, -1, LANES), "section", split_axis=0, concat_axis=0, tiled=True
+    ).reshape(sec_n, -1)
     fg = got[:, :span].astype(jnp.float32) + got[:, span:2 * span].astype(jnp.float32)
     fg = fg.reshape(1, channels, length)
     ig = got[:, 2 * span:3 * span].reshape(channels, length)
-    tg = jnp.moveaxis(joined(got[:, 3 * span:]).reshape(sec_n, 3, 7, sub), 0, 2)
+    tg = jnp.moveaxis(joined(got[:, 3 * span:3 * span + 63 * sub]).reshape(sec_n, 3, 7, sub), 0, 2)
     tg = tg.reshape(1, 3, 7, channels)
     ig = lax.all_to_all(ig, "ctx", split_axis=1, concat_axis=0, tiled=True)
     return (ig[None], fg, tg)

time: 123 us -> 117 us (0.951)
  local copies, waits for them, and re-layouts: 11 us -> 6.34 us
  other arithmetic: 6.66 us -> 5.24 us
    unnamed x14 -> x10, local copies, waits for them, and re-layouts: 6.77 us -> 2.71 us
    all_to_all x1 -> x0, other arithmetic: 1.28 us -> none  [shards(): lax.all_to_all(sent, 'section', split_axis=0, concat_axis=0, tiled=True)]
where the time goes in v4:
time: 117 us; the launch traced here: 116 us
  waiting for transfers between devices  37.6 us (32%)
  starting transfers between devices  25.8 us (22%)
  Pallas kernels  24.6 us (21%)
  blocking collectives  15.8 us (14%)
  local copies, waits for them, and re-layouts  6.34 us (5%)
  other arithmetic  5.24 us (4%)
    pallas_call x1, Pallas kernels, run_chain(): pl.pallas_call(lambda *refs: chain_kernel(sub, *refs), out_shape=(jax.Sha...  24.6 us
    all_to_all x1, starting transfers between devices, shards(): lax.all_to_all(sent, 'ctx', split_axis=0, concat_axis=2, tiled=True)[0]  16.6 us
    all_to_all x1, blocking collectives, shards(): lax.all_to_all(sent.reshape(sec_n, -1, LANES), 'section', split_axis=0, c...  15.8 us
    all_to_all x1, waiting for transfers between devices, shards(): lax.all_to_all(sent, 'ctx', split_axis=0, concat_axis=2, tiled=True)[0]  14.6 us
    all_to_all x1, waiting for transfers between devices, shards(): ig = lax.all_to_all(ig, 'ctx', split_axis=1, concat_axis=0, tiled=True)  13 us
    all_to_all x1, waiting for transfers between devices, shards(): lax.all_to_all(sent, 'section', split_axis=0, concat_axis=0, tiled=True)  10.1 us
    all_to_all x1, starting transfers between devices, shards(): ig = lax.all_to_all(ig, 'ctx', split_axis=1, concat_axis=0, tiled=True)  4.95 us
    all_to_all x1, starting transfers between devices, shards(): lax.all_to_all(sent, 'section', split_axis=0, concat_axis=0, tiled=True)  4.3 us
  transfers between devices with their start and end apart: 3, of which 3 were waited for; matrix products, arithmetic and copies ran while one was open for 4% of the time, Pallas kernels for 0%

profile of v4, /device:TPU:8, one launch (start us, length us, event | category | flops | bytes accessed | tf_op | source)
XLA Modules:
  0.0 116.3 jit_solution(504203239694224531)
XLA Ops:
  0.7 0.9 copy-done
  1.6 1.7 %pad_maximum_fusion.1 = bf16[64,18,128]{2,1,0:T(8,128)(2,1)} fusion(bf16[64,2,128]{2,1,0:T(2,128)(2,1)S(1)} %dynamic-slice_bitcast_fusion, bf16[64,16,128]{2,1,0:T(8,128)(2,1)} %bitcast.55), kind=kLoop, calls=%fused_computation.7 | loop fusion | flops 589824 | bytes 589824 | tf_op jit(solution)/shard_map/concatenate | solution.py:260
  3.4 16.6 %all-to-all-start = ((bf16[64,18,128]{2,1,0:T(8,128)(2,1)}), bf16[64,18,128]{2,1,0:T(8,128)(2,1)S(1)}, u32[]{:S(2)}, u32[]{:S(2)}) async-start(bf16[64,18,128]{2,1,0:T(8,128)(2,1)} %pad_maximum_fusion.1), calls=%async_computation | async-start | bytes 786432 | tf_op jit(solution)/shard_map/all_to_all | solution.py:261
  20.0 0.8 constant_dynamic-slice_fusion
  20.7 0.1 copy.87
  20.8 0.1 copy.75
  21.2 0.1 reshape_squeeze.7
  21.3 0.3 fusion.35
  21.6 0.1 sine_negate_fusion.1
  21.7 0.3 fusion.31
  22.0 0.3 fusion.29
  22.3 14.6 %all-to-all-done = bf16[64,18,128]{2,1,0:T(8,128)(2,1)S(1)} async-done(((bf16[64,18,128]{2,1,0:T(8,128)(2,1)}), bf16[64,18,128]{2,1,0:T(8,128)(2,1)S(1)}, u32[]{:S(2)}, u32[]{:S(2)}) %all-to-all-start) | async-done | bytes 294944 | tf_op jit(solution)/shard_map/all_to_all | solution.py:261
  36.9 0.8 pad_maximum_fusion
  37.8 4.3 %all-to-all-start.1 = ((bf16[8,257,128]{2,1,0:T(8,128)(2,1)}), bf16[8,257,128]{2,1,0:T(8,128)(2,1)S(1)}, u32[]{:S(2)}, u32[]{:S(2)}) async-start(bf16[8,257,128]{2,1,0:T(8,128)(2,1)} %pad_maximum_fusion), calls=%async_computation.1 | async-start | bytes 1081344 | tf_op jit(solution)/shard_map/all_to_all | solution.py:277
  42.1 0.3 sine_negate_fusion
  42.5 10.1 %all-to-all-done.1 = bf16[8,257,128]{2,1,0:T(8,128)(2,1)S(1)} async-done(((bf16[8,257,128]{2,1,0:T(8,128)(2,1)}), bf16[8,257,128]{2,1,0:T(8,128)(2,1)S(1)}, u32[]{:S(2)}, u32[]{:S(2)}) %all-to-all-start.1) | async-done | bytes 526368 | tf_op jit(solution)/shard_map/all_to_all | solution.py:277
  52.8 24.6 %hyena_chain.1 = (bf16[8,128,128]{2,1,0:T(8,128)(2,1)S(1)}, f32[8,128,128]{2,1,0:T(8,128)S(1)}, f32[8,42,8,128]{3,2,1,0:T(8,128)S(1)}) custom-call(f32[336]{0:T(512)S(1)} %reshape_reshape.9.refs_0_, bf16[8,128,128]{2,1,0:T(8,128)(2,1)S(1)} %get-tuple-element.28.refs_1_, bf16[8,128,128]{2,1,0:T(8,128)(2,1)S(1)} %get-tuple-element.27.refs_2_, ...), custom_call_target="tpu_custom_call" | custom-call | tf_op jit(solution)/shard_map/hyena_chain/pallas_call | solution.py:208
  77.5 0.2 copy.97
  77.6 0.3 reduce-precision_convert_fusion
  78.0 0.6 reduce_sum.9
  78.7 0.1 copy.80
  78.8 15.8 %all_to_all.41 = bf16[8,385,128]{2,1,0:T(8,128)(2,1)S(1)} all-to-all(bf16[8,385,128]{2,1,0:T(8,128)(2,1)S(1)} %copy.80), channel_id=1, replica_groups=mesh['section'=8,'ctx'=64] {'section'}, dimensions={0} | all-to-all | bytes 1576960 | tf_op jit(solution)/shard_map/all_to_all | solution.py:289
  94.6 0.1 copy.96
  94.8 0.1 all_to_all.34
  94.9 0.9 copy.81
  95.8 5.0 %all-to-all-start.3 = ((bf16[16,64,128]{2,0,1:T(8,128)(2,1)}), bf16[16,64,128]{2,0,1:T(8,128)(2,1)S(1)}, u32[]{:S(2)}, u32[]{:S(2)}) async-start(bf16[16,64,128]{2,0,1:T(8,128)(2,1)} %copy.81), calls=%async_computation.3 | async-start | bytes 524288 | tf_op jit(solution)/shard_map/all_to_all | solution.py:297
  100.9 0.1 copy.82
  101.0 0.1 copy.83
  101.1 0.7 copy.84
  101.8 0.9 reshape.56
  102.7 13.0 %all-to-all-done.3 = bf16[16,64,128]{2,0,1:T(8,128)(2,1)S(1)} async-done(((bf16[16,64,128]{2,0,1:T(8,128)(2,1)}), bf16[16,64,128]{2,0,1:T(8,128)(2,1)S(1)}, u32[]{:S(2)}, u32[]{:S(2)}) %all-to-all-start.3) | async-done | bytes 262176 | tf_op jit(solution)/shard_map/all_to_all | solution.py:297
  115.6 0.7 copy.100
  (28 shorter events, 1.0 us)
Async XLA Ops:
  0.6 1.0 copy-start
  0.6 20.5 %copy-start.1 = (bf16[1,16,8192]{2,1,0:T(8,128)(2,1)S(1)}, bf16[1,16,8192]{2,1,0:T(8,128)(2,1)}, u32[]{:S(2)}) copy-start(bf16[1,16,8192]{2,1,0:T(8,128)(2,1)} %param.6) | copy-start | bytes 786436
  3.4 33.5 %all-to-all-start = ((bf16[64,18,128]{2,1,0:T(8,128)(2,1)}), bf16[64,18,128]{2,1,0:T(8,128)(2,1)S(1)}, u32[]{:S(2)}, u32[]{:S(2)}) async-start(bf16[64,18,128]{2,1,0:T(8,128)(2,1)} %pad_maximum_fusion.1), calls=%async_computation | async-start | bytes 786432 | tf_op jit(solution)/shard_map/all_to_all | solution.py:261
  37.8 14.8 %all-to-all-start.1 = ((bf16[8,257,128]{2,1,0:T(8,128)(2,1)}), bf16[8,257,128]{2,1,0:T(8,128)(2,1)S(1)}, u32[]{:S(2)}, u32[]{:S(2)}) async-start(bf16[8,257,128]{2,1,0:T(8,128)(2,1)} %pad_maximum_fusion), calls=%async_computation.1 | async-start | bytes 1081344 | tf_op jit(solution)/shard_map/all_to_all | solution.py:277
  95.8 19.9 %all-to-all-start.3 = ((bf16[16,64,128]{2,0,1:T(8,128)(2,1)}), bf16[16,64,128]{2,0,1:T(8,128)(2,1)S(1)}, u32[]{:S(2)}, u32[]{:S(2)}) async-start(bf16[16,64,128]{2,0,1:T(8,128)(2,1)} %copy.81), calls=%async_computation.3 | async-start | bytes 524288 | tf_op jit(solution)/shard_map/all_to_all | solution.py:297

commit v5 on v4

--- a/solution.py
+++ b/solution.py
@@ -286,16 +286,18 @@
         [fg_high, fg_low, in_all.reshape(sec_n, span), taps_out],
         axis=1,
     )
-    got = lax.all_to_all(
+    got3 = lax.all_to_all(
         sent.reshape(sec_n, -1, LANES), "section", split_axis=0, concat_axis=0, tiled=True
-    ).reshape(sec_n, -1)
+    )
+    got = got3.reshape(sec_n, -1)
     fg = got[:, :span].astype(jnp.float32) + got[:, span:2 * span].astype(jnp.float32)
     fg = fg.reshape(1, channels, length)
-    ig = got[:, 2 * span:3 * span].reshape(channels, length)
+    ig = got3[:, 2 * rows:3 * rows].reshape(sec_n, sub, ctx_n, tok_dev)
+    ig = jnp.transpose(ig, (2, 0, 1, 3)).reshape(ctx_n, channels, tok_dev)
     tg = jnp.moveaxis(joined(got[:, 3 * span:3 * span + 63 * sub]).reshape(sec_n, 3, 7, sub), 0, 2)
     tg = tg.reshape(1, 3, 7, channels)
-    ig = lax.all_to_all(ig, "ctx", split_axis=1, concat_axis=0, tiled=True)
-    return (ig[None], fg, tg)
+    ig = lax.all_to_all(ig, "ctx", split_axis=0, concat_axis=0, tiled=True)
+    return (ig.reshape(1, ctx_n * channels, tok_dev), fg, tg)
 
 
 def solution(mesh):

time: 117 us -> 117 us (level)
  no operation moved by 1% of the time
where the time goes in v5:
time: 117 us; the launch traced here: 116 us
  waiting for transfers between devices  37.5 us (32%)
  starting transfers between devices  25.8 us (22%)
  Pallas kernels  24.6 us (21%)
  blocking collectives  15.8 us (14%)
  local copies, waits for them, and re-layouts  6.22 us (5%)
  other arithmetic  5.24 us (4%)
    pallas_call x1, Pallas kernels, run_chain(): pl.pallas_call(lambda *refs: chain_kernel(sub, *refs), out_shape=(jax.Sha...  24.6 us
    all_to_all x1, starting transfers between devices, shards(): lax.all_to_all(sent, 'ctx', split_axis=0, concat_axis=2, tiled=True)[0]  16.6 us
    all_to_all x1, blocking collectives, shards(): lax.all_to_all(sent.reshape(sec_n, -1, LANES), 'section', split_axis=0, c...  15.8 us
    all_to_all x1, waiting for transfers between devices, shards(): lax.all_to_all(sent, 'ctx', split_axis=0, concat_axis=2, tiled=True)[0]  14.6 us
    all_to_all x1, waiting for transfers between devices, shards(): ig = lax.all_to_all(ig, 'ctx', split_axis=0, concat_axis=0, tiled=True)  12.9 us
    all_to_all x1, waiting for transfers between devices, shards(): lax.all_to_all(sent, 'section', split_axis=0, concat_axis=0, tiled=True)  10.1 us
    all_to_all x1, starting transfers between devices, shards(): ig = lax.all_to_all(ig, 'ctx', split_axis=0, concat_axis=0, tiled=True)  4.95 us
    all_to_all x1, starting transfers between devices, shards(): lax.all_to_all(sent, 'section', split_axis=0, concat_axis=0, tiled=True)  4.3 us
  transfers between devices with their start and end apart: 3, of which 3 were waited for; matrix products, arithmetic and copies ran while one was open for 4% of the time, Pallas kernels for 0%

profile of v5, /device:TPU:8, one launch (start us, length us, event | category | flops | bytes accessed | tf_op | source)
XLA Modules:
  0.0 116.1 jit_solution(15693971438793000998)
XLA Ops:
  0.7 0.9 copy-done
  1.6 1.7 %pad_maximum_fusion.1 = bf16[64,18,128]{2,1,0:T(8,128)(2,1)} fusion(bf16[64,2,128]{2,1,0:T(2,128)(2,1)S(1)} %dynamic-slice_bitcast_fusion, bf16[64,16,128]{2,1,0:T(8,128)(2,1)} %bitcast.58), kind=kLoop, calls=%fused_computation.7 | loop fusion | flops 589824 | bytes 589824 | tf_op jit(solution)/shard_map/concatenate | solution.py:260
  3.4 16.6 %all-to-all-start = ((bf16[64,18,128]{2,1,0:T(8,128)(2,1)}), bf16[64,18,128]{2,1,0:T(8,128)(2,1)S(1)}, u32[]{:S(2)}, u32[]{:S(2)}) async-start(bf16[64,18,128]{2,1,0:T(8,128)(2,1)} %pad_maximum_fusion.1), calls=%async_computation | async-start | bytes 786432 | tf_op jit(solution)/shard_map/all_to_all | solution.py:261
  20.0 0.8 constant_dynamic-slice_fusion
  20.7 0.1 copy.65
  20.8 0.1 copy.53
  21.2 0.1 reshape_squeeze.7
  21.3 0.3 fusion.35
  21.6 0.1 sine_negate_fusion.1
  21.7 0.3 fusion.31
  22.0 0.3 fusion.29
  22.3 14.6 %all-to-all-done = bf16[64,18,128]{2,1,0:T(8,128)(2,1)S(1)} async-done(((bf16[64,18,128]{2,1,0:T(8,128)(2,1)}), bf16[64,18,128]{2,1,0:T(8,128)(2,1)S(1)}, u32[]{:S(2)}, u32[]{:S(2)}) %all-to-all-start) | async-done | bytes 294944 | tf_op jit(solution)/shard_map/all_to_all | solution.py:261
  36.9 0.8 pad_maximum_fusion
  37.8 4.3 %all-to-all-start.1 = ((bf16[8,257,128]{2,1,0:T(8,128)(2,1)}), bf16[8,257,128]{2,1,0:T(8,128)(2,1)S(1)}, u32[]{:S(2)}, u32[]{:S(2)}) async-start(bf16[8,257,128]{2,1,0:T(8,128)(2,1)} %pad_maximum_fusion), calls=%async_computation.1 | async-start | bytes 1081344 | tf_op jit(solution)/shard_map/all_to_all | solution.py:277
  42.1 0.3 sine_negate_fusion
  42.5 10.1 %all-to-all-done.1 = bf16[8,257,128]{2,1,0:T(8,128)(2,1)S(1)} async-done(((bf16[8,257,128]{2,1,0:T(8,128)(2,1)}), bf16[8,257,128]{2,1,0:T(8,128)(2,1)S(1)}, u32[]{:S(2)}, u32[]{:S(2)}) %all-to-all-start.1) | async-done | bytes 526368 | tf_op jit(solution)/shard_map/all_to_all | solution.py:277
  52.7 0.1 reshape_reshape.9.refs_0_
  52.8 24.6 %hyena_chain.1 = (bf16[8,128,128]{2,1,0:T(8,128)(2,1)S(1)}, f32[8,128,128]{2,1,0:T(8,128)S(1)}, f32[8,42,8,128]{3,2,1,0:T(8,128)S(1)}) custom-call(f32[336]{0:T(512)S(1)} %reshape_reshape.9.refs_0_, bf16[8,128,128]{2,1,0:T(8,128)(2,1)S(1)} %get-tuple-element.22.refs_1_, bf16[8,128,128]{2,1,0:T(8,128)(2,1)S(1)} %get-tuple-element.21.refs_2_, ...), custom_call_target="tpu_custom_call" | custom-call | tf_op jit(solution)/shard_map/hyena_chain/pallas_call | solution.py:208
  77.5 0.2 copy.75
  77.6 0.3 reduce-precision_convert_fusion
  78.0 0.6 reduce_sum.9
  78.7 0.1 copy.58
  78.8 15.8 %all_to_all.30 = bf16[8,385,128]{2,1,0:T(8,128)(2,1)S(1)} all-to-all(bf16[8,385,128]{2,1,0:T(8,128)(2,1)S(1)} %copy.58), channel_id=1, replica_groups=mesh['section'=8,'ctx'=64] {'section'}, dimensions={0} | all-to-all | bytes 1576960 | tf_op jit(solution)/shard_map/all_to_all | solution.py:289
  94.6 0.9 copy.59
  95.5 5.0 %all-to-all-start.3 = ((bf16[64,16,128]{2,1,0:T(8,128)(2,1)}), bf16[64,16,128]{2,1,0:T(8,128)(2,1)S(1)}, u32[]{:S(2)}, u32[]{:S(2)}) async-start(bf16[64,16,128]{2,1,0:T(8,128)(2,1)} %copy.59), calls=%async_computation.3 | async-start | bytes 524288 | tf_op jit(solution)/shard_map/all_to_all | solution.py:299
  100.5 0.1 copy.74
  100.7 0.9 reshape.62
  101.6 0.1 copy.60
  101.7 0.1 copy.61
  101.8 0.7 copy.62
  102.5 12.9 %all-to-all-done.3 = bf16[64,16,128]{2,1,0:T(8,128)(2,1)S(1)} async-done(((bf16[64,16,128]{2,1,0:T(8,128)(2,1)}), bf16[64,16,128]{2,1,0:T(8,128)(2,1)S(1)}, u32[]{:S(2)}, u32[]{:S(2)}) %all-to-all-start.3) | async-done | bytes 262176 | tf_op jit(solution)/shard_map/all_to_all | solution.py:299
  115.4 0.7 copy.78
  (27 shorter events, 0.9 us)
Async XLA Ops:
  0.6 1.0 copy-start
  0.6 20.5 %copy-start.1 = (bf16[1,16,8192]{2,1,0:T(8,128)(2,1)S(1)}, bf16[1,16,8192]{2,1,0:T(8,128)(2,1)}, u32[]{:S(2)}) copy-start(bf16[1,16,8192]{2,1,0:T(8,128)(2,1)} %param.6) | copy-start | bytes 786436
  3.4 33.5 %all-to-all-start = ((bf16[64,18,128]{2,1,0:T(8,128)(2,1)}), bf16[64,18,128]{2,1,0:T(8,128)(2,1)S(1)}, u32[]{:S(2)}, u32[]{:S(2)}) async-start(bf16[64,18,128]{2,1,0:T(8,128)(2,1)} %pad_maximum_fusion.1), calls=%async_computation | async-start | bytes 786432 | tf_op jit(solution)/shard_map/all_to_all | solution.py:261
  37.8 14.8 %all-to-all-start.1 = ((bf16[8,257,128]{2,1,0:T(8,128)(2,1)}), bf16[8,257,128]{2,1,0:T(8,128)(2,1)S(1)}, u32[]{:S(2)}, u32[]{:S(2)}) async-start(bf16[8,257,128]{2,1,0:T(8,128)(2,1)} %pad_maximum_fusion), calls=%async_computation.1 | async-start | bytes 1081344 | tf_op jit(solution)/shard_map/all_to_all | solution.py:277
  95.5 19.9 %all-to-all-start.3 = ((bf16[64,16,128]{2,1,0:T(8,128)(2,1)}), bf16[64,16,128]{2,1,0:T(8,128)(2,1)S(1)}, u32[]{:S(2)}, u32[]{:S(2)}) async-start(bf16[64,16,128]{2,1,0:T(8,128)(2,1)} %copy.59), calls=%async_computation.3 | async-start | bytes 524288 | tf_op jit(solution)/shard_map/all_to_all | solution.py:299

commit v6 on v5

--- a/solution.py
+++ b/solution.py
@@ -70,7 +70,7 @@
 
 def chain_kernel(
     sub, taps_ref, x_ref, h_ref, og_ref, a1h, a1l, tcr, tsr, w2h, w2l, wbh, wbl, a3h, a3l,
-    in_ref, fg_ref, tp_ref, q_s, k_s, v_s, conv_s, hs_s, ws_s, ds_s,
+    in_ref, fg_ref, tp_ref, q_s, k_s, v_s, conv_s, hs_s, ws_s, ds_s, xs_s,
 ):
     layers, rows, lanes = x_ref.shape
     half = rows // sub
@@ -83,12 +83,17 @@
         first_row = first_row | (row_id == c * half)
         last_row = last_row | (row_id == c * half + half - 1)
 
-    def fft(signal):
+    def fft(signal, exact=False):
         twc = tcr[...]
         tws = tsr[...]
         parts = []
         for c in range(sub):
-            y = dot_left(a1h[...], a1l[...], signal[c * half:(c + 1) * half, :])
+            piece = signal[c * half:(c + 1) * half, :]
+            if exact:
+                v_hi = piece.astype(jnp.bfloat16)
+                y = mat(a1h[...], v_hi) + mat(a1l[...], v_hi)
+            else:
+                y = dot_left(a1h[...], a1l[...], piece)
             yr, yi = y[:blocks], y[blocks:]
             parts.append(jnp.concatenate([yr * twc + yi * tws, yi * twc - yr * tws], axis=1))
         return dot_right(jnp.concatenate(parts, axis=0), w2h[...], w2l[...])
@@ -136,13 +141,14 @@
         feats = [jnp.zeros((rows, lanes), jnp.float32) for _ in range(3)]
         for j in range(7):
             xs = back(x, j)
+            xs_s[layer * 7 + j] = xs
             for i in range(3):
                 feats[i] = feats[i] + tap(layer, i, j) * xs
         q, k, v = [f.astype(jnp.bfloat16).astype(jnp.float32) for f in feats]
         q_s[layer] = q
         k_s[layer] = k
         v_s[layer] = v
-        hspec = fft(h_ref[layer].astype(jnp.float32))
+        hspec = fft(h_ref[layer], exact=True)
         wspec = fft(k * v)
         hs_s[layer] = hspec
         ws_s[layer] = wspec
@@ -171,9 +177,8 @@
             summed = summed + ahead(term, j)
         rounded = summed.astype(jnp.bfloat16)
         in_ref[layer] = rounded
-        x = x_ref[layer].astype(jnp.float32)
         for j in range(7):
-            xs = back(x, j)
+            xs = xs_s[layer * 7 + j]
             for i in range(3):
                 prod = grads[i] * xs
                 for c in range(sub):
@@ -214,7 +219,9 @@
         ),
         in_specs=[pl.BlockSpec(memory_space=pltpu.SMEM)] + [vmem] * 13,
         out_specs=(vmem, vmem, vmem),
-        scratch_shapes=[sig_shape] * 4 + [spec_shape] * 3,
+        scratch_shapes=[sig_shape] * 4
+        + [spec_shape] * 3
+        + [pltpu.VMEM((layers * 7, rows, LANES), jnp.float32)],
         compiler_params=pltpu.CompilerParams(vmem_limit_bytes=48 * 1024 * 1024),
         name="hyena_chain",
     )(

time: 117 us -> 117 us (level)
  no operation moved by 1% of the time
where the time goes in v6:
time: 117 us; the launch traced here: 116 us
  waiting for transfers between devices  37.5 us (32%)
  starting transfers between devices  25.8 us (22%)
  Pallas kernels  24.6 us (21%)
  blocking collectives  15.8 us (14%)
  local copies, waits for them, and re-layouts  6.22 us (5%)
  other arithmetic  5.24 us (4%)
    pallas_call x1, Pallas kernels, run_chain(): pl.pallas_call(lambda *refs: chain_kernel(sub, *refs), out_shape=(jax.Sha...  24.6 us
    all_to_all x1, starting transfers between devices, shards(): lax.all_to_all(sent, 'ctx', split_axis=0, concat_axis=2, tiled=True)[0]  16.6 us
    all_to_all x1, blocking collectives, shards(): lax.all_to_all(sent.reshape(sec_n, -1, LANES), 'section', split_axis=0, c...  15.8 us
    all_to_all x1, waiting for transfers between devices, shards(): lax.all_to_all(sent, 'ctx', split_axis=0, concat_axis=2, tiled=True)[0]  14.6 us
    all_to_all x1, waiting for transfers between devices, shards(): ig = lax.all_to_all(ig, 'ctx', split_axis=0, concat_axis=0, tiled=True)  12.9 us
    all_to_all x1, waiting for transfers between devices, shards(): lax.all_to_all(sent, 'section', split_axis=0, concat_axis=0, tiled=True)  10.1 us
    all_to_all x1, starting transfers between devices, shards(): ig = lax.all_to_all(ig, 'ctx', split_axis=0, concat_axis=0, tiled=True)  4.95 us
    all_to_all x1, starting transfers between devices, shards(): lax.all_to_all(sent, 'section', split_axis=0, concat_axis=0, tiled=True)  4.3 us
  transfers between devices with their start and end apart: 3, of which 3 were waited for; matrix products, arithmetic and copies ran while one was open for 4% of the time, Pallas kernels for 0%

profile of v6, /device:TPU:8, one launch (start us, length us, event | category | flops | bytes accessed | tf_op | source)
XLA Modules:
  0.0 116.1 jit_solution(9687927253813703430)
XLA Ops:
  0.7 0.9 copy-done
  1.6 1.7 %pad_maximum_fusion.1 = bf16[64,18,128]{2,1,0:T(8,128)(2,1)} fusion(bf16[64,2,128]{2,1,0:T(2,128)(2,1)S(1)} %dynamic-slice_bitcast_fusion, bf16[64,16,128]{2,1,0:T(8,128)(2,1)} %bitcast.58), kind=kLoop, calls=%fused_computation.7 | loop fusion | flops 589824 | bytes 589824 | tf_op jit(solution)/shard_map/concatenate | solution.py:267
  3.4 16.6 %all-to-all-start = ((bf16[64,18,128]{2,1,0:T(8,128)(2,1)}), bf16[64,18,128]{2,1,0:T(8,128)(2,1)S(1)}, u32[]{:S(2)}, u32[]{:S(2)}) async-start(bf16[64,18,128]{2,1,0:T(8,128)(2,1)} %pad_maximum_fusion.1), calls=%async_computation | async-start | bytes 786432 | tf_op jit(solution)/shard_map/all_to_all | solution.py:268
  20.0 0.8 constant_dynamic-slice_fusion
  20.7 0.1 copy.65
  20.8 0.1 copy.53
  21.2 0.1 reshape_squeeze.7
  21.3 0.3 fusion.35
  21.6 0.1 sine_negate_fusion.1
  21.7 0.3 fusion.31
  22.0 0.3 fusion.29
  22.3 14.6 %all-to-all-done = bf16[64,18,128]{2,1,0:T(8,128)(2,1)S(1)} async-done(((bf16[64,18,128]{2,1,0:T(8,128)(2,1)}), bf16[64,18,128]{2,1,0:T(8,128)(2,1)S(1)}, u32[]{:S(2)}, u32[]{:S(2)}) %all-to-all-start) | async-done | bytes 294944 | tf_op jit(solution)/shard_map/all_to_all | solution.py:268
  36.9 0.8 pad_maximum_fusion
  37.8 4.3 %all-to-all-start.1 = ((bf16[8,257,128]{2,1,0:T(8,128)(2,1)}), bf16[8,257,128]{2,1,0:T(8,128)(2,1)S(1)}, u32[]{:S(2)}, u32[]{:S(2)}) async-start(bf16[8,257,128]{2,1,0:T(8,128)(2,1)} %pad_maximum_fusion), calls=%async_computation.1 | async-start | bytes 1081344 | tf_op jit(solution)/shard_map/all_to_all | solution.py:284
  42.1 0.3 sine_negate_fusion
  42.5 10.1 %all-to-all-done.1 = bf16[8,257,128]{2,1,0:T(8,128)(2,1)S(1)} async-done(((bf16[8,257,128]{2,1,0:T(8,128)(2,1)}), bf16[8,257,128]{2,1,0:T(8,128)(2,1)S(1)}, u32[]{:S(2)}, u32[]{:S(2)}) %all-to-all-start.1) | async-done | bytes 526368 | tf_op jit(solution)/shard_map/all_to_all | solution.py:284
  52.7 0.1 reshape_reshape.9.refs_0_
  52.8 24.6 %hyena_chain.1 = (bf16[8,128,128]{2,1,0:T(8,128)(2,1)S(1)}, f32[8,128,128]{2,1,0:T(8,128)S(1)}, f32[8,42,8,128]{3,2,1,0:T(8,128)S(1)}) custom-call(f32[336]{0:T(512)S(1)} %reshape_reshape.9.refs_0_, bf16[8,128,128]{2,1,0:T(8,128)(2,1)S(1)} %get-tuple-element.22.refs_1_, bf16[8,128,128]{2,1,0:T(8,128)(2,1)S(1)} %get-tuple-element.21.refs_2_, ...), custom_call_target="tpu_custom_call" | custom-call | tf_op jit(solution)/shard_map/hyena_chain/pallas_call | solution.py:213
  77.5 0.2 copy.75
  77.6 0.3 reduce-precision_convert_fusion
  77.9 0.6 reduce_sum.9
  78.7 0.1 copy.58
  78.8 15.8 %all_to_all.30 = bf16[8,385,128]{2,1,0:T(8,128)(2,1)S(1)} all-to-all(bf16[8,385,128]{2,1,0:T(8,128)(2,1)S(1)} %copy.58), channel_id=1, replica_groups=mesh['section'=8,'ctx'=64] {'section'}, dimensions={0} | all-to-all | bytes 1576960 | tf_op jit(solution)/shard_map/all_to_all | solution.py:296
  94.6 0.9 copy.59
  95.5 5.0 %all-to-all-start.3 = ((bf16[64,16,128]{2,1,0:T(8,128)(2,1)}), bf16[64,16,128]{2,1,0:T(8,128)(2,1)S(1)}, u32[]{:S(2)}, u32[]{:S(2)}) async-start(bf16[64,16,128]{2,1,0:T(8,128)(2,1)} %copy.59), calls=%async_computation.3 | async-start | bytes 524288 | tf_op jit(solution)/shard_map/all_to_all | solution.py:306
  100.5 0.1 copy.74
  100.7 0.9 reshape.62
  101.6 0.1 copy.60
  101.7 0.1 copy.61
  101.8 0.7 copy.62
  102.5 12.9 %all-to-all-done.3 = bf16[64,16,128]{2,1,0:T(8,128)(2,1)S(1)} async-done(((bf16[64,16,128]{2,1,0:T(8,128)(2,1)}), bf16[64,16,128]{2,1,0:T(8,128)(2,1)S(1)}, u32[]{:S(2)}, u32[]{:S(2)}) %all-to-all-start.3) | async-done | bytes 262176 | tf_op jit(solution)/shard_map/all_to_all | solution.py:306
  115.4 0.7 copy.78
  (27 shorter events, 0.9 us)
Async XLA Ops:
  0.6 1.0 copy-start
  0.6 20.5 %copy-start.1 = (bf16[1,16,8192]{2,1,0:T(8,128)(2,1)S(1)}, bf16[1,16,8192]{2,1,0:T(8,128)(2,1)}, u32[]{:S(2)}) copy-start(bf16[1,16,8192]{2,1,0:T(8,128)(2,1)} %param.6) | copy-start | bytes 786436
  3.4 33.5 %all-to-all-start = ((bf16[64,18,128]{2,1,0:T(8,128)(2,1)}), bf16[64,18,128]{2,1,0:T(8,128)(2,1)S(1)}, u32[]{:S(2)}, u32[]{:S(2)}) async-start(bf16[64,18,128]{2,1,0:T(8,128)(2,1)} %pad_maximum_fusion.1), calls=%async_computation | async-start | bytes 786432 | tf_op jit(solution)/shard_map/all_to_all | solution.py:268
  37.8 14.8 %all-to-all-start.1 = ((bf16[8,257,128]{2,1,0:T(8,128)(2,1)}), bf16[8,257,128]{2,1,0:T(8,128)(2,1)S(1)}, u32[]{:S(2)}, u32[]{:S(2)}) async-start(bf16[8,257,128]{2,1,0:T(8,128)(2,1)} %pad_maximum_fusion), calls=%async_computation.1 | async-start | bytes 1081344 | tf_op jit(solution)/shard_map/all_to_all | solution.py:284
  95.5 19.9 %all-to-all-start.3 = ((bf16[64,16,128]{2,1,0:T(8,128)(2,1)}), bf16[64,16,128]{2,1,0:T(8,128)(2,1)S(1)}, u32[]{:S(2)}, u32[]{:S(2)}) async-start(bf16[64,16,128]{2,1,0:T(8,128)(2,1)} %copy.59), calls=%async_computation.3 | async-start | bytes 524288 | tf_op jit(solution)/shard_map/all_to_all | solution.py:306

commit v7 on v5

--- a/solution.py
+++ b/solution.py
@@ -151,7 +151,7 @@
         conv_s[layer] = ifft(jnp.concatenate([hr * wr - hi * wi, hr * wi + hi * wr], axis=1))
         return carry
 
-    lax.fori_loop(0, layers, phase_one, 0)
+    lax.fori_loop(0, layers, phase_one, 0, unroll=2)
 
     def phase_two(step, carried):
         layer = layers - 1 - step
@@ -192,7 +192,7 @@
         fg_ref[layer] = ifft(jnp.concatenate([wr * dr + wi * di, wr * di - wi * dr], axis=1))
         return carry
 
-    lax.fori_loop(0, layers, phase_three, 0)
+    lax.fori_loop(0, layers, phase_three, 0, unroll=2)
 
 
 def run_chain(x_all, h_all, og, taps_all):

time: 117 us -> 115 us (0.983)
  Pallas kernels: 24.6 us -> 23.4 us
    pallas_call x1, Pallas kernels: 24.6 us -> 23.4 us  [run_chain(): pl.pallas_call(lambda *refs: chain_kernel(sub, *refs), out_shape=(jax.Sha...]
where the time goes in v7:
time: 115 us
  waiting for transfers between devices  37.5 us (33%)
  starting transfers between devices  25.8 us (22%)
  Pallas kernels  23.4 us (20%)
  blocking collectives  15.8 us (14%)
  local copies, waits for them, and re-layouts  6.22 us (5%)
  other arithmetic  5.24 us (5%)
    pallas_call x1, Pallas kernels, run_chain(): pl.pallas_call(lambda *refs: chain_kernel(sub, *refs), out_shape=(jax.Sha...  23.4 us
    all_to_all x1, starting transfers between devices, shards(): lax.all_to_all(sent, 'ctx', split_axis=0, concat_axis=2, tiled=True)[0]  16.6 us
    all_to_all x1, blocking collectives, shards(): lax.all_to_all(sent.reshape(sec_n, -1, LANES), 'section', split_axis=0, c...  15.8 us
    all_to_all x1, waiting for transfers between devices, shards(): lax.all_to_all(sent, 'ctx', split_axis=0, concat_axis=2, tiled=True)[0]  14.6 us
    all_to_all x1, waiting for transfers between devices, shards(): ig = lax.all_to_all(ig, 'ctx', split_axis=0, concat_axis=0, tiled=True)  12.9 us
    all_to_all x1, waiting for transfers between devices, shards(): lax.all_to_all(sent, 'section', split_axis=0, concat_axis=0, tiled=True)  10.1 us
    all_to_all x1, starting transfers between devices, shards(): ig = lax.all_to_all(ig, 'ctx', split_axis=0, concat_axis=0, tiled=True)  4.95 us
    all_to_all x1, starting transfers between devices, shards(): lax.all_to_all(sent, 'section', split_axis=0, concat_axis=0, tiled=True)  4.3 us
  transfers between devices with their start and end apart: 3, of which 3 were waited for; matrix products, arithmetic and copies ran while one was open for 4% of the time, Pallas kernels for 0%

profile of v7, /device:TPU:8, one launch (start us, length us, event | category | flops | bytes accessed | tf_op | source)
XLA Modules:
  0.0 114.9 jit_solution(297743317112911776)
XLA Ops:
  0.7 0.9 copy-done
  1.6 1.7 %pad_maximum_fusion.1 = bf16[64,18,128]{2,1,0:T(8,128)(2,1)} fusion(bf16[64,2,128]{2,1,0:T(2,128)(2,1)S(1)} %dynamic-slice_bitcast_fusion, bf16[64,16,128]{2,1,0:T(8,128)(2,1)} %bitcast.58), kind=kLoop, calls=%fused_computation.7 | loop fusion | flops 589824 | bytes 589824 | tf_op jit(solution)/shard_map/concatenate | solution.py:260
  3.4 16.6 %all-to-all-start = ((bf16[64,18,128]{2,1,0:T(8,128)(2,1)}), bf16[64,18,128]{2,1,0:T(8,128)(2,1)S(1)}, u32[]{:S(2)}, u32[]{:S(2)}) async-start(bf16[64,18,128]{2,1,0:T(8,128)(2,1)} %pad_maximum_fusion.1), calls=%async_computation | async-start | bytes 786432 | tf_op jit(solution)/shard_map/all_to_all | solution.py:261
  20.0 0.8 constant_dynamic-slice_fusion
  20.7 0.1 copy.65
  20.8 0.1 copy.53
  21.2 0.1 reshape_squeeze.7
  21.3 0.3 fusion.35
  21.6 0.1 sine_negate_fusion.1
  21.7 0.3 fusion.31
  22.0 0.3 fusion.29
  22.3 14.6 %all-to-all-done = bf16[64,18,128]{2,1,0:T(8,128)(2,1)S(1)} async-done(((bf16[64,18,128]{2,1,0:T(8,128)(2,1)}), bf16[64,18,128]{2,1,0:T(8,128)(2,1)S(1)}, u32[]{:S(2)}, u32[]{:S(2)}) %all-to-all-start) | async-done | bytes 294944 | tf_op jit(solution)/shard_map/all_to_all | solution.py:261
  36.9 0.8 pad_maximum_fusion
  37.8 4.3 %all-to-all-start.1 = ((bf16[8,257,128]{2,1,0:T(8,128)(2,1)}), bf16[8,257,128]{2,1,0:T(8,128)(2,1)S(1)}, u32[]{:S(2)}, u32[]{:S(2)}) async-start(bf16[8,257,128]{2,1,0:T(8,128)(2,1)} %pad_maximum_fusion), calls=%async_computation.1 | async-start | bytes 1081344 | tf_op jit(solution)/shard_map/all_to_all | solution.py:277
  42.1 0.3 sine_negate_fusion
  42.5 10.1 %all-to-all-done.1 = bf16[8,257,128]{2,1,0:T(8,128)(2,1)S(1)} async-done(((bf16[8,257,128]{2,1,0:T(8,128)(2,1)}), bf16[8,257,128]{2,1,0:T(8,128)(2,1)S(1)}, u32[]{:S(2)}, u32[]{:S(2)}) %all-to-all-start.1) | async-done | bytes 526368 | tf_op jit(solution)/shard_map/all_to_all | solution.py:277
  52.7 0.1 reshape_reshape.9.refs_0_
  52.8 23.4 %hyena_chain.1 = (bf16[8,128,128]{2,1,0:T(8,128)(2,1)S(1)}, f32[8,128,128]{2,1,0:T(8,128)S(1)}, f32[8,42,8,128]{3,2,1,0:T(8,128)S(1)}) custom-call(f32[336]{0:T(512)S(1)} %reshape_reshape.9.refs_0_, bf16[8,128,128]{2,1,0:T(8,128)(2,1)S(1)} %get-tuple-element.22.refs_1_, bf16[8,128,128]{2,1,0:T(8,128)(2,1)S(1)} %get-tuple-element.21.refs_2_, ...), custom_call_target="tpu_custom_call" | custom-call | tf_op jit(solution)/shard_map/hyena_chain/pallas_call | solution.py:208
  76.3 0.2 copy.75
  76.4 0.3 reduce-precision_convert_fusion
  76.8 0.6 reduce_sum.9
  77.5 0.1 copy.58
  77.6 15.8 %all_to_all.30 = bf16[8,385,128]{2,1,0:T(8,128)(2,1)S(1)} all-to-all(bf16[8,385,128]{2,1,0:T(8,128)(2,1)S(1)} %copy.58), channel_id=1, replica_groups=mesh['section'=8,'ctx'=64] {'section'}, dimensions={0} | all-to-all | bytes 1576960 | tf_op jit(solution)/shard_map/all_to_all | solution.py:289
  93.5 0.9 copy.59
  94.3 5.0 %all-to-all-start.3 = ((bf16[64,16,128]{2,1,0:T(8,128)(2,1)}), bf16[64,16,128]{2,1,0:T(8,128)(2,1)S(1)}, u32[]{:S(2)}, u32[]{:S(2)}) async-start(bf16[64,16,128]{2,1,0:T(8,128)(2,1)} %copy.59), calls=%async_computation.3 | async-start | bytes 524288 | tf_op jit(solution)/shard_map/all_to_all | solution.py:299
  99.3 0.1 copy.74
  99.5 0.9 reshape.62
  100.4 0.1 copy.60
  100.5 0.1 copy.61
  100.6 0.7 copy.62
  101.3 12.9 %all-to-all-done.3 = bf16[64,16,128]{2,1,0:T(8,128)(2,1)S(1)} async-done(((bf16[64,16,128]{2,1,0:T(8,128)(2,1)}), bf16[64,16,128]{2,1,0:T(8,128)(2,1)S(1)}, u32[]{:S(2)}, u32[]{:S(2)}) %all-to-all-start.3) | async-done | bytes 262176 | tf_op jit(solution)/shard_map/all_to_all | solution.py:299
  114.2 0.7 copy.78
  (27 shorter events, 0.9 us)
Async XLA Ops:
  0.6 1.0 copy-start
  0.6 20.5 %copy-start.1 = (bf16[1,16,8192]{2,1,0:T(8,128)(2,1)S(1)}, bf16[1,16,8192]{2,1,0:T(8,128)(2,1)}, u32[]{:S(2)}) copy-start(bf16[1,16,8192]{2,1,0:T(8,128)(2,1)} %param.6) | copy-start | bytes 786436
  3.4 33.5 %all-to-all-start = ((bf16[64,18,128]{2,1,0:T(8,128)(2,1)}), bf16[64,18,128]{2,1,0:T(8,128)(2,1)S(1)}, u32[]{:S(2)}, u32[]{:S(2)}) async-start(bf16[64,18,128]{2,1,0:T(8,128)(2,1)} %pad_maximum_fusion.1), calls=%async_computation | async-start | bytes 786432 | tf_op jit(solution)/shard_map/all_to_all | solution.py:261
  37.8 14.8 %all-to-all-start.1 = ((bf16[8,257,128]{2,1,0:T(8,128)(2,1)}), bf16[8,257,128]{2,1,0:T(8,128)(2,1)S(1)}, u32[]{:S(2)}, u32[]{:S(2)}) async-start(bf16[8,257,128]{2,1,0:T(8,128)(2,1)} %pad_maximum_fusion), calls=%async_computation.1 | async-start | bytes 1081344 | tf_op jit(solution)/shard_map/all_to_all | solution.py:277
  94.3 19.9 %all-to-all-start.3 = ((bf16[64,16,128]{2,1,0:T(8,128)(2,1)}), bf16[64,16,128]{2,1,0:T(8,128)(2,1)S(1)}, u32[]{:S(2)}, u32[]{:S(2)}) async-start(bf16[64,16,128]{2,1,0:T(8,128)(2,1)} %copy.59), calls=%async_computation.3 | async-start | bytes 524288 | tf_op jit(solution)/shard_map/all_to_all | solution.py:299

commit v8 on v7

--- a/solution.py
+++ b/solution.py
@@ -151,7 +151,7 @@
         conv_s[layer] = ifft(jnp.concatenate([hr * wr - hi * wi, hr * wi + hi * wr], axis=1))
         return carry
 
-    lax.fori_loop(0, layers, phase_one, 0, unroll=2)
+    lax.fori_loop(0, layers, phase_one, 0, unroll=4)
 
     def phase_two(step, carried):
         layer = layers - 1 - step
@@ -184,7 +184,7 @@
                     tp_ref[layer, row] = part
         return rounded.astype(jnp.float32)
 
-    lax.fori_loop(0, layers, phase_two, og_ref[...].astype(jnp.float32))
+    lax.fori_loop(0, layers, phase_two, og_ref[...].astype(jnp.float32), unroll=2)
 
     def phase_three(layer, carry):
         wr, wi = real_imag(ws_s[layer])
@@ -192,7 +192,7 @@
         fg_ref[layer] = ifft(jnp.concatenate([wr * dr + wi * di, wr * di - wi * dr], axis=1))
         return carry
 
-    lax.fori_loop(0, layers, phase_three, 0, unroll=2)
+    lax.fori_loop(0, layers, phase_three, 0, unroll=4)
 
 
 def run_chain(x_all, h_all, og, taps_all):

time: 115 us -> 114 us (level)
  Pallas kernels: 23.4 us -> 21.9 us
    pallas_call x1, Pallas kernels: 23.4 us -> 21.9 us  [run_chain(): pl.pallas_call(lambda *refs: chain_kernel(sub, *refs), out_shape=(jax.Sha...]
where the time goes in v8:
time: 114 us; the launch traced here: 113 us
  waiting for transfers between devices  37.5 us (33%)
  starting transfers between devices  25.8 us (23%)
  Pallas kernels  21.9 us (19%)
  blocking collectives  15.8 us (14%)
  local copies, waits for them, and re-layouts  6.22 us (5%)
  other arithmetic  5.24 us (5%)
    pallas_call x1, Pallas kernels, run_chain(): pl.pallas_call(lambda *refs: chain_kernel(sub, *refs), out_shape=(jax.Sha...  21.9 us
    all_to_all x1, starting transfers between devices, shards(): lax.all_to_all(sent, 'ctx', split_axis=0, concat_axis=2, tiled=True)[0]  16.6 us
    all_to_all x1, blocking collectives, shards(): lax.all_to_all(sent.reshape(sec_n, -1, LANES), 'section', split_axis=0, c...  15.8 us
    all_to_all x1, waiting for transfers between devices, shards(): lax.all_to_all(sent, 'ctx', split_axis=0, concat_axis=2, tiled=True)[0]  14.6 us
    all_to_all x1, waiting for transfers between devices, shards(): ig = lax.all_to_all(ig, 'ctx', split_axis=0, concat_axis=0, tiled=True)  12.8 us
    all_to_all x1, waiting for transfers between devices, shards(): lax.all_to_all(sent, 'section', split_axis=0, concat_axis=0, tiled=True)  10.1 us
    all_to_all x1, starting transfers between devices, shards(): ig = lax.all_to_all(ig, 'ctx', split_axis=0, concat_axis=0, tiled=True)  4.96 us
    all_to_all x1, starting transfers between devices, shards(): lax.all_to_all(sent, 'section', split_axis=0, concat_axis=0, tiled=True)  4.3 us
  transfers between devices with their start and end apart: 3, of which 3 were waited for; matrix products, arithmetic and copies ran while one was open for 4% of the time, Pallas kernels for 0%

profile of v8, /device:TPU:8, one launch (start us, length us, event | category | flops | bytes accessed | tf_op | source)
XLA Modules:
  0.0 113.4 jit_solution(812760032351111631)
XLA Ops:
  0.7 0.9 copy-done
  1.6 1.7 %pad_maximum_fusion.1 = bf16[64,18,128]{2,1,0:T(8,128)(2,1)} fusion(bf16[64,2,128]{2,1,0:T(2,128)(2,1)S(1)} %dynamic-slice_bitcast_fusion, bf16[64,16,128]{2,1,0:T(8,128)(2,1)} %bitcast.58), kind=kLoop, calls=%fused_computation.7 | loop fusion | flops 589824 | bytes 589824 | tf_op jit(solution)/shard_map/concatenate | solution.py:260
  3.4 16.6 %all-to-all-start = ((bf16[64,18,128]{2,1,0:T(8,128)(2,1)}), bf16[64,18,128]{2,1,0:T(8,128)(2,1)S(1)}, u32[]{:S(2)}, u32[]{:S(2)}) async-start(bf16[64,18,128]{2,1,0:T(8,128)(2,1)} %pad_maximum_fusion.1), calls=%async_computation | async-start | bytes 786432 | tf_op jit(solution)/shard_map/all_to_all | solution.py:261
  20.0 0.8 constant_dynamic-slice_fusion
  20.7 0.1 copy.65
  20.8 0.1 copy.53
  21.2 0.1 reshape_squeeze.7
  21.3 0.3 fusion.35
  21.6 0.1 sine_negate_fusion.1
  21.7 0.3 fusion.31
  22.0 0.3 fusion.29
  22.3 14.6 %all-to-all-done = bf16[64,18,128]{2,1,0:T(8,128)(2,1)S(1)} async-done(((bf16[64,18,128]{2,1,0:T(8,128)(2,1)}), bf16[64,18,128]{2,1,0:T(8,128)(2,1)S(1)}, u32[]{:S(2)}, u32[]{:S(2)}) %all-to-all-start) | async-done | bytes 294944 | tf_op jit(solution)/shard_map/all_to_all | solution.py:261
  36.9 0.8 pad_maximum_fusion
  37.8 4.3 %all-to-all-start.1 = ((bf16[8,257,128]{2,1,0:T(8,128)(2,1)}), bf16[8,257,128]{2,1,0:T(8,128)(2,1)S(1)}, u32[]{:S(2)}, u32[]{:S(2)}) async-start(bf16[8,257,128]{2,1,0:T(8,128)(2,1)} %pad_maximum_fusion), calls=%async_computation.1 | async-start | bytes 1081344 | tf_op jit(solution)/shard_map/all_to_all | solution.py:277
  42.1 0.3 sine_negate_fusion
  42.5 10.1 %all-to-all-done.1 = bf16[8,257,128]{2,1,0:T(8,128)(2,1)S(1)} async-done(((bf16[8,257,128]{2,1,0:T(8,128)(2,1)}), bf16[8,257,128]{2,1,0:T(8,128)(2,1)S(1)}, u32[]{:S(2)}, u32[]{:S(2)}) %all-to-all-start.1) | async-done | bytes 526368 | tf_op jit(solution)/shard_map/all_to_all | solution.py:277
  52.7 0.1 reshape_reshape.9.refs_0_
  52.8 21.9 %hyena_chain.1 = (bf16[8,128,128]{2,1,0:T(8,128)(2,1)S(1)}, f32[8,128,128]{2,1,0:T(8,128)S(1)}, f32[8,42,8,128]{3,2,1,0:T(8,128)S(1)}) custom-call(f32[336]{0:T(512)S(1)} %reshape_reshape.9.refs_0_, bf16[8,128,128]{2,1,0:T(8,128)(2,1)S(1)} %get-tuple-element.22.refs_1_, bf16[8,128,128]{2,1,0:T(8,128)(2,1)S(1)} %get-tuple-element.21.refs_2_, ...), custom_call_target="tpu_custom_call" | custom-call | tf_op jit(solution)/shard_map/hyena_chain/pallas_call | solution.py:208
  74.8 0.2 copy.75
  75.0 0.3 reduce-precision_convert_fusion
  75.3 0.6 reduce_sum.9
  76.0 0.1 copy.58
  76.1 15.8 %all_to_all.30 = bf16[8,385,128]{2,1,0:T(8,128)(2,1)S(1)} all-to-all(bf16[8,385,128]{2,1,0:T(8,128)(2,1)S(1)} %copy.58), channel_id=1, replica_groups=mesh['section'=8,'ctx'=64] {'section'}, dimensions={0} | all-to-all | bytes 1576960 | tf_op jit(solution)/shard_map/all_to_all | solution.py:289
  92.0 0.9 copy.59
  92.9 5.0 %all-to-all-start.3 = ((bf16[64,16,128]{2,1,0:T(8,128)(2,1)}), bf16[64,16,128]{2,1,0:T(8,128)(2,1)S(1)}, u32[]{:S(2)}, u32[]{:S(2)}) async-start(bf16[64,16,128]{2,1,0:T(8,128)(2,1)} %copy.59), calls=%async_computation.3 | async-start | bytes 524288 | tf_op jit(solution)/shard_map/all_to_all | solution.py:299
  97.8 0.1 copy.74
  98.0 0.9 reshape.62
  98.9 0.1 copy.60
  99.1 0.1 copy.61
  99.2 0.7 copy.62
  99.9 12.8 %all-to-all-done.3 = bf16[64,16,128]{2,1,0:T(8,128)(2,1)S(1)} async-done(((bf16[64,16,128]{2,1,0:T(8,128)(2,1)}), bf16[64,16,128]{2,1,0:T(8,128)(2,1)S(1)}, u32[]{:S(2)}, u32[]{:S(2)}) %all-to-all-start.3) | async-done | bytes 262176 | tf_op jit(solution)/shard_map/all_to_all | solution.py:299
  112.7 0.7 copy.78
  (27 shorter events, 0.9 us)
Async XLA Ops:
  0.6 1.0 copy-start
  0.6 20.5 %copy-start.1 = (bf16[1,16,8192]{2,1,0:T(8,128)(2,1)S(1)}, bf16[1,16,8192]{2,1,0:T(8,128)(2,1)}, u32[]{:S(2)}) copy-start(bf16[1,16,8192]{2,1,0:T(8,128)(2,1)} %param.6) | copy-start | bytes 786436
  3.4 33.5 %all-to-all-start = ((bf16[64,18,128]{2,1,0:T(8,128)(2,1)}), bf16[64,18,128]{2,1,0:T(8,128)(2,1)S(1)}, u32[]{:S(2)}, u32[]{:S(2)}) async-start(bf16[64,18,128]{2,1,0:T(8,128)(2,1)} %pad_maximum_fusion.1), calls=%async_computation | async-start | bytes 786432 | tf_op jit(solution)/shard_map/all_to_all | solution.py:261
  37.8 14.8 %all-to-all-start.1 = ((bf16[8,257,128]{2,1,0:T(8,128)(2,1)}), bf16[8,257,128]{2,1,0:T(8,128)(2,1)S(1)}, u32[]{:S(2)}, u32[]{:S(2)}) async-start(bf16[8,257,128]{2,1,0:T(8,128)(2,1)} %pad_maximum_fusion), calls=%async_computation.1 | async-start | bytes 1081344 | tf_op jit(solution)/shard_map/all_to_all | solution.py:277
  92.9 19.9 %all-to-all-start.3 = ((bf16[64,16,128]{2,1,0:T(8,128)(2,1)}), bf16[64,16,128]{2,1,0:T(8,128)(2,1)S(1)}, u32[]{:S(2)}, u32[]{:S(2)}) async-start(bf16[64,16,128]{2,1,0:T(8,128)(2,1)} %copy.59), calls=%async_computation.3 | async-start | bytes 524288 | tf_op jit(solution)/shard_map/all_to_all | solution.py:299
